TPU v7x, 32 devices: a whole 2x2x4 slice. The times are simulated.
32 devices in a mesh: parts: 2 (over y), blk: 4 (over z), grp: 2 (over x), fld: 2 (over core).
Axes of the slice: x: 2, y: 2, z: 4, core: 2. Of those that a mesh axis runs over, the one named last changes fastest.
Arguments:
- coords: float32 [32, 2, 2, 128], P(('parts', 'blk'), 'grp'), parts along dimension 0, may hold values from 0 to 1
- fields: float32 [32, 2, 64, 128], P(('parts', 'blk'), 'grp', 'fld'), parts along dimension 0, may hold values from -6 to 6
- neighbours: int32 [32, 2, 4], P(('parts', 'blk'), 'grp'), parts along dimension 0, may hold values from -1 to 29, as said below
Outputs:
- whitened: float32 [32, 2, 64, 128], P(('parts', 'blk'), 'grp', 'fld'), parts along dimension 0
- precision_product: float32 [32, 2, 64, 128], P(('parts', 'blk'), 'grp', 'fld'), parts along dimension 0
There are 2 independent parts, one for each index of `parts`. A program takes and returns all parts, laid end to end along the dimension named above; each array names one. Nothing has to cross between parts.
Inputs may be any that keep to these rules, and one draw needn't show every extreme that they name: `neighbours`: each entry is -1 or the flat id j * 2 + h of a block with i - 8 <= j <= i - 1 and |h - g| <= 1, where (i, g) is the listing block; the ids of one list differ.
All inputs are finite; a program needn't handle non-finite values.
Results may differ from a plain program's by a relative error of at most 0.0003.
Values sent between devices are 32-bit elements; how exact they have to be, the bound alone decides.
No kernel may reach another device: no remote copies, remote signals or barrier semaphores. Data moves between devices by JAX's collectives and lax.ppermute only.
A program may use at most 64 MiB of HBM per device.

v0:
```python
import jax
import jax.numpy as jnp
from jax import lax
from jax.sharding import PartitionSpec as P
from jax.experimental import pallas as pl

ELL = 0.3
NUGGET = 0.25


def padded_2(cells, sides, width):
    for axis, dim in sides:
        count = lax.axis_size(axis)
        ends = count - 1
        head = lax.slice_in_dim(cells, 0, width, axis=dim)
        tail = lax.slice_in_dim(cells, cells.shape[dim] - width, cells.shape[dim], axis=dim)
        cells = jnp.concatenate(
            [
                lax.ppermute(tail, axis, [(i, (i + 1) % count) for i in range(ends)]),
                cells,
                lax.ppermute(head, axis, [((i + 1) % count, i) for i in range(ends)]),
            ],
            axis=dim,
        )
    return cells


def shifted(block, axis, distance):
    devices = range(lax.axis_size(axis))
    route = [(i - distance, i) for i in devices if i - distance in devices]
    return lax.ppermute(block, axis, route)


def _diag_kernel(a_ref, u_ref, li_ref):
    g_count, n, _ = a_ref.shape
    rows = n // 8
    sub = lax.broadcasted_iota(jnp.int32, (8, n), 0)
    lane = lax.broadcasted_iota(jnp.int32, (8, n), 1)
    lefts, rights, scales = [], [], []
    for g in range(g_count):
        lefts.append([a_ref[g, 8 * r : 8 * r + 8, :] for r in range(rows)])
        rights.append(
            [jnp.where(lane == sub + 8 * r, 1.0, 0.0).astype(jnp.float32) for r in range(rows)]
        )
        scales.append([jnp.zeros((8, n), jnp.float32) for r in range(rows)])
    for j in range(n):
        r0, s = divmod(j, 8)
        for g in range(g_count):
            left, right, scale = lefts[g], rights[g], scales[g]
            row_l = jnp.broadcast_to(left[r0][s : s + 1, :], (8, n))
            row_r = jnp.broadcast_to(right[r0][s : s + 1, :], (8, n))
            piv = jnp.broadcast_to(row_l[:, j : j + 1], (8, n))
            inv = 1.0 / piv
            scale[r0] = jnp.where(sub == s, lax.rsqrt(piv), scale[r0])
            for r in range(r0, rows):
                f = jnp.broadcast_to(left[r][:, j : j + 1], (8, n)) * inv
                new_l = left[r] - f * row_l
                new_r = right[r] - f * row_r
                if r == r0:
                    new_l = jnp.where(sub > s, new_l, left[r])
                    new_r = jnp.where(sub > s, new_r, right[r])
                left[r] = new_l
                right[r] = new_r
    for g in range(g_count):
        for r in range(rows):
            upper = jnp.where(lane >= sub + 8 * r, lefts[g][r], 0.0)
            u_ref[g, 8 * r : 8 * r + 8, :] = upper * scales[g][r]
            li_ref[g, 8 * r : 8 * r + 8, :] = rights[g][r] * scales[g][r]


def diag_factor(a):
    shape = jax.ShapeDtypeStruct(a.shape, jnp.float32)
    return pl.pallas_call(_diag_kernel, out_shape=(shape, shape))(a)


def mm(spec, x, y):
    return jnp.einsum(spec, x, y, precision=lax.Precision.HIGHEST)


def many_blocks(pts, vals, mask):
    groups, slots, _, points = pts.shape
    count = slots * points
    fields = vals.shape[2]
    coords = jnp.transpose(pts, (0, 1, 3, 2)).reshape(groups, count, 2)
    mpts = jnp.repeat(mask, points, axis=1)
    delta_x = coords[:, :, 0][:, :, None] - coords[:, :, 0][:, None, :]
    delta_y = coords[:, :, 1][:, :, None] - coords[:, :, 1][:, None, :]
    scaled = jnp.sqrt(3.0) * jnp.sqrt(delta_x * delta_x + delta_y * delta_y) / ELL
    kernel = (1.0 + scaled) * jnp.exp(-scaled)
    eye = jnp.eye(count, dtype=jnp.float32)
    cov = mpts[:, :, None] * mpts[:, None, :] * kernel + eye * (NUGGET * mpts + 1.0 - mpts)[:, :, None]
    values = jnp.transpose(vals, (0, 1, 3, 2)).reshape(groups, count, fields) * mpts[:, :, None]
    trail = cov
    rest = values
    panels, inverses = [], []
    for k in range(slots):
        _, inv = diag_factor(trail[:, :points, :points])
        inverses.append(inv)
        white = mm("gij,gjf->gif", inv, rest[:, :points])
        if k < slots - 1:
            panel = mm("gic,gjc->gij", trail[:, points:, :points], inv)
            panels.append(panel)
            trail = trail[:, points:, points:] - mm("gic,gjc->gij", panel, panel)
            rest = rest[:, points:] - mm("gic,gcf->gif", panel, white)
    back = mm("gji,gjf->gif", inverses[-1], white)
    for k in range(slots - 2, -1, -1):
        rhs = -mm("gic,gif->gcf", panels[k], back)
        back = jnp.concatenate([mm("gji,gjf->gif", inverses[k], rhs), back], axis=1)
    back = back * mpts[:, :, None]
    back = jnp.transpose(back.reshape(groups, slots, points, fields), (0, 1, 3, 2))
    return jnp.transpose(white, (0, 2, 1)), back


def fetch_across(local):
    return padded_2(local, (("grp", 1),), 1)


def fetch_older(local):
    older = []
    for distance in (2, 1):
        older.append(shifted(local, "blk", distance))
    return jnp.concatenate(older + [local], axis=0)


def back_across(terms):
    total_count = terms[:, 1:2]
    for column, offset in ((0, -1), (2, 1)):
        total_count = total_count + shifted(terms[:, column : column + 1], "grp", offset)
    return total_count


def back_older(terms):
    per = terms.shape[0] // 3
    farthest = terms[:per]
    nearest = terms[per : 2 * per]
    total_count = terms[2 * per :]
    for distance, piece in ((1, nearest), (2, farthest)):
        total_count = total_count + shifted(piece, "blk", -distance)
    return total_count


def per_device(coords, fields, neighbours):
    per = coords.shape[0]
    window_coords = fetch_older(fetch_across(coords))
    window_fields = fetch_older(fetch_across(fields))
    groups = lax.axis_size("grp")
    blk_pos = lax.axis_index("blk")
    grp_pos = lax.axis_index("grp")
    neighbour_lists = neighbours.reshape(per, neighbours.shape[2])
    earlier = neighbour_lists // groups - (blk_pos - 2) * per
    beside = neighbour_lists % groups - grp_pos + 1
    own_slot = ((2 * per + jnp.arange(per, dtype=jnp.int32)) * 3 + 1)[:, None]
    slots = jnp.concatenate(
        [jnp.where(neighbour_lists >= 0, earlier * 3 + beside, own_slot), own_slot], axis=1
    )
    masks = jnp.concatenate(
        [(neighbour_lists >= 0).astype(jnp.float32), jnp.ones((per, 1), jnp.float32)], axis=1
    )
    flat_coords = window_coords.reshape((9 * per,) + coords.shape[2:])
    flat_fields = window_fields.reshape((9 * per,) + fields.shape[2:])
    width = slots.shape[1]
    local_fields = fields.shape[2]
    points = fields.shape[3]
    whitened, backs = many_blocks(flat_coords[slots], flat_fields[slots], masks)
    onehot = (slots.reshape(-1)[None, :] == jnp.arange(9 * per, dtype=jnp.int32)[:, None]).astype(
        jnp.float32
    )
    onehot = onehot * masks.reshape(-1)[None, :]
    terms = jnp.dot(
        onehot, backs.reshape(width * per, local_fields * points), precision=lax.Precision.HIGHEST
    )
    terms = terms.reshape(3 * per, 3, local_fields, points)
    product = back_across(back_older(terms))
    return (whitened[:, None], product)


def solution(mesh):
    return jax.shard_map(
        per_device,
        mesh=mesh,
        in_specs=(
            P(("parts", "blk"), "grp", None, None),
            P(("parts", "blk"), "grp", "fld", None),
            P(("parts", "blk"), "grp", None),
        ),
        out_specs=(
            P(("parts", "blk"), "grp", "fld", None),
            P(("parts", "blk"), "grp", "fld", None),
        ),
        check_vma=False,
    )
```

profile of v0, /device:TPU:0, one launch (start us, length us, event | category | flops | bytes accessed | tf_op | source)
XLA Modules:
  0.0 212.8 jit_solution(5708720816856170593)
XLA Ops:
  0.6 4.8 %collective-permute-start = (f32[4,1,2,128]{3,2,1,0:T(2,128)}, f32[4,1,2,128]{3,2,1,0:T(2,128)S(1)}, u32[]{:S(2)}, u32[]{:S(2)}) collective-permute-start(f32[4,1,2,128]{3,2,1,0:T(2,128)} %param.3), channel_id=1, source_target_pairs={{0,2},{1,3},{4,6},{5,7},{8,10},{9,11},{12,14},{13,15},{16,18},{17,... | collective-permute-start | bytes 12296 | tf_op jit(solution)/shard_map/ppermute | solution.py:19
  5.5 1.3 collective-permute-start.1
  6.8 5.2 %collective-permute-start.4 = (f32[4,1,32,128]{3,2,1,0:T(8,128)}, f32[4,1,32,128]{3,2,1,0:T(8,128)}, u32[]{:S(2)}, u32[]{:S(2)}) collective-permute-start(f32[4,1,32,128]{3,2,1,0:T(8,128)} %param.4), channel_id=1, source_target_pairs={{0,2},{1,3},{4,6},{5,7},{8,10},{9,11},{12,14},{13,15},{16,18},{17,... | collective-permute-start | bytes 196616 | tf_op jit(solution)/shard_map/ppermute | solution.py:19
  11.9 1.3 collective-permute-start.5
  13.4 0.7 broadcast_compare_fusion
  14.1 0.8 fusion.101
  14.8 0.8 fusion.41
  15.9 0.7 constant_dynamic-update-slice_fusion.1
  16.6 3.5 %collective-permute-start.3 = (f32[4,3,2,128]{3,2,1,0:T(2,128)S(1)}, f32[4,3,2,128]{3,2,1,0:T(2,128)S(1)}, u32[]{:S(2)}, u32[]{:S(2)}) collective-permute-start(f32[4,3,2,128]{3,2,1,0:T(2,128)S(1)} %constant_dynamic-update-slice_fusion), channel_id=1, source_target_pairs={{0,4},{4,8},{8,12},{1,5},{5,9},{9,13},{2,6},{6,10},{10,14},{3,7},{... | collective-permute-start | bytes 36872 | tf_op jit(solution)/shard_map/ppermute | solution.py:31
  20.1 4.5 %collective-permute-start.2 = (f32[4,3,2,128]{3,2,1,0:T(2,128)S(1)}, f32[4,3,2,128]{3,2,1,0:T(2,128)S(1)}, u32[]{:S(2)}, u32[]{:S(2)}) collective-permute-start(f32[4,3,2,128]{3,2,1,0:T(2,128)S(1)} %constant_dynamic-update-slice_fusion), channel_id=1, source_target_pairs={{0,8},{4,12},{1,9},{5,13},{2,10},{6,14},{3,11},{7,15},{16,24},{20,... | collective-permute-start | bytes 36872 | tf_op jit(solution)/shard_map/ppermute | solution.py:31
  26.6 5.3 %multiply_add_fusion = f32[4,640,640]{2,1,0:T(8,128)S(1)} fusion(f32[4,640]{1,0:T(4,128)S(1)} %get-tuple-element.18, f32[640,640]{1,0:T(8,128)S(1)} %fusion, f32[4,640]{1,0:T(4,128)S(1)} %get-tuple-element.27, f32[4,640]{1,0:T(4,128)S(1)} %get-tuple-element.28, f32[4,640]{1,0:T(4,128)S(1)} %get-tuple-element.19), kind=kLoop, calls=%fused_computation.2 | loop fusion | flops 21299200 | bytes 8232960 | tf_op jit(solution)/shard_map/add | solution.py:91
  31.9 2.7 %copy-done = f32[4,640,640]{2,1,0:T(8,128)} copy-done((f32[4,640,640]{2,1,0:T(8,128)}, f32[4,640,640]{2,1,0:T(8,128)S(1)}, u32[]{:S(2)}) %copy-start) | copy-done | bytes 6553624
  34.7 0.7 slice.134.a_ref
  35.4 19.2 %shard_map.50 = (f32[4,128,128]{2,1,0:T(8,128)}, f32[4,128,128]{2,1,0:T(8,128)}) custom-call(f32[4,128,128]{2,1,0:T(8,128)} %slice.134.a_ref), custom_call_target="tpu_custom_call" | custom-call | tf_op jit(solution)/shard_map/pallas_call | solution.py:73
  54.5 2.3 %fusion.1 = f32[4,512,128]{2,1,0:T(8,128)S(1)} fusion(f32[4,128,128]{2,1,0:T(8,128)} %get-tuple-element.7, f32[4,640,640]{2,1,0:T(8,128)} %copy-done), kind=kOutput, calls=%fused_computation.18 | convolution fusion | flops 402653184 | bytes 2359296 | tf_op jit(solution)/shard_map/gic,gjc->gij/dot_general | solution.py:77
  56.9 5.7 %slice_subtract_fusion = f32[4,512,512]{2,1,0:T(8,128)S(1)} fusion(f32[4,640,640]{2,1,0:T(8,128)} %copy-done, f32[4,512,128]{2,1,0:T(8,128)S(1)} %fusion.1), kind=kOutput, calls=%fused_computation.3 | convolution fusion | flops 1611661312 | bytes 10485760 | tf_op jit(solution)/shard_map/gic,gjc->gij/dot_general | solution.py:77
  62.6 2.0 copy-done.1
  64.6 0.7 slice.137.a_ref
  65.3 19.1 %shard_map.51 = (f32[4,128,128]{2,1,0:T(8,128)}, f32[4,128,128]{2,1,0:T(8,128)}) custom-call(f32[4,128,128]{2,1,0:T(8,128)} %slice.137.a_ref), custom_call_target="tpu_custom_call" | custom-call | tf_op jit(solution)/shard_map/pallas_call | solution.py:73
  84.5 2.0 fusion.3
  86.5 4.0 %slice_subtract_fusion.1 = f32[4,384,384]{2,1,0:T(8,128)S(1)} fusion(f32[4,512,512]{2,1,0:T(8,128)} %copy-done.1, f32[4,384,128]{2,1,0:T(8,128)S(1)} %fusion.3), kind=kOutput, calls=%fused_computation.4 | convolution fusion | flops 906559488 | bytes 6291456 | tf_op jit(solution)/shard_map/gic,gjc->gij/dot_general | solution.py:77
  90.5 1.4 copy-done.2
  91.9 0.7 slice.140.a_ref
  92.6 19.2 %shard_map.52 = (f32[4,128,128]{2,1,0:T(8,128)}, f32[4,128,128]{2,1,0:T(8,128)}) custom-call(f32[4,128,128]{2,1,0:T(8,128)} %slice.140.a_ref), custom_call_target="tpu_custom_call" | custom-call | tf_op jit(solution)/shard_map/pallas_call | solution.py:73
  111.8 2.1 fusion.5
  113.9 2.3 %convolution_subtract_fusion = f32[4,256,256]{2,1,0:T(8,128)S(1)} fusion(f32[4,256,128]{2,1,0:T(8,128)S(1)} %fusion.5, f32[4,384,384]{2,1,0:T(8,128)} %copy-done.2), kind=kOutput, calls=%fused_computation.7 | convolution fusion | flops 402915328 | bytes 3145728 | tf_op jit(solution)/shard_map/gic,gjc->gij/dot_general | solution.py:77
  116.2 1.0 copy-done.3
  117.2 0.7 slice.143.a_ref
  117.9 19.2 %shard_map.53 = (f32[4,128,128]{2,1,0:T(8,128)}, f32[4,128,128]{2,1,0:T(8,128)}) custom-call(f32[4,128,128]{2,1,0:T(8,128)} %slice.143.a_ref), custom_call_target="tpu_custom_call" | custom-call | tf_op jit(solution)/shard_map/pallas_call | solution.py:73
  137.1 1.7 fusion.7
  138.8 1.5 constant_dynamic-update-slice_fusion.5
  141.5 2.1 %collective-permute-start.7 = (f32[4,3,32,128]{3,2,1,0:T(8,128)}, f32[4,3,32,128]{3,2,1,0:T(8,128)}, u32[]{:S(2)}, u32[]{:S(2)}) collective-permute-start(f32[4,3,32,128]{3,2,1,0:T(8,128)} %constant_dynamic-update-slice_fusion.3), channel_id=1, source_target_pairs={{0,4},{4,8},{8,12},{1,5},{5,9},{9,13},{2,6},{6,10},{10,14},{3,7},{... | collective-permute-start | bytes 589832 | tf_op jit(solution)/shard_map/ppermute | solution.py:31
  143.7 5.7 %collective-permute-start.6 = (f32[4,3,32,128]{3,2,1,0:T(8,128)}, f32[4,3,32,128]{3,2,1,0:T(8,128)}, u32[]{:S(2)}, u32[]{:S(2)}) collective-permute-start(f32[4,3,32,128]{3,2,1,0:T(8,128)} %constant_dynamic-update-slice_fusion.3), channel_id=1, source_target_pairs={{0,8},{4,12},{1,9},{5,13},{2,10},{6,14},{3,11},{7,15},{16,24},{20,... | collective-permute-start | bytes 589832 | tf_op jit(solution)/shard_map/ppermute | solution.py:31
  149.4 2.3 %convolution_subtract_fusion.1.a_ref = f32[4,128,128]{2,1,0:T(8,128)} fusion(f32[4,128,128]{2,1,0:T(8,128)S(1)} %fusion.7, f32[4,256,256]{2,1,0:T(8,128)} %copy-done.3), kind=kOutput, calls=%fused_computation.8 | convolution fusion | flops 100728832 | bytes 1048576 | tf_op jit(solution)/shard_map/gic,gjc->gij/dot_general | solution.py:77
  151.8 19.1 %shard_map.54 = (f32[4,128,128]{2,1,0:T(8,128)}, f32[4,128,128]{2,1,0:T(8,128)}) custom-call(f32[4,128,128]{2,1,0:T(8,128)} %convolution_subtract_fusion.1.a_ref), custom_call_target="tpu_custom_call" | custom-call | tf_op jit(solution)/shard_map/pallas_call | solution.py:73
  170.9 2.0 pad_maximum_fusion
  172.9 2.5 %gather_fusion.1 = f32[20,32,128]{2,1,0:T(8,128)} fusion(f32[36,32,128]{2,1,0:T(8,128)} %bitcast.98, s32[1024]{0:T(1024)} %copy-done.11), kind=kCustom, calls=%fused_computation.1 | custom fusion | bytes 655440 | tf_op jit(solution)/shard_map/gather | solution.py:164
  175.4 1.1 bitcast_multiply_fusion
  176.9 1.3 convolution_subtract_fusion.2
  178.8 1.0 convolution_subtract_fusion.3
  181.0 1.5 fusion.25
  186.3 0.7 convolution_negate_fusion
  188.8 1.3 collective-permute-start.9
  190.1 1.3 collective-permute-start.8
  191.5 9.6 %collective-permute-done.9 = f32[4,3,32,128]{3,2,1,0:T(8,128)S(1)} collective-permute-done((f32[4,3,32,128]{3,2,1,0:T(8,128)S(1)}, f32[4,3,32,128]{3,2,1,0:T(8,128)S(1)}, u32[]{:S(2)}, u32[]{:S(2)}) %collective-permute-start.9) | collective-permute-done | bytes 196640 | tf_op jit(solution)/shard_map/ppermute | solution.py:31
  201.2 4.5 %collective-permute-start.11 = (f32[4,1,32,128]{3,2,1,0:T(8,128)S(1)}, f32[4,1,32,128]{3,2,1,0:T(8,128)S(1)}, u32[]{:S(2)}, u32[]{:S(2)}) collective-permute-start(f32[4,1,32,128]{3,2,1,0:T(8,128)S(1)} %get-tuple-element.24), channel_id=1, source_target_pairs={{0,2},{1,3},{4,6},{5,7},{8,10},{9,11},{12,14},{13,15},{16,18},{17,... | collective-permute-start | bytes 196616 | tf_op jit(solution)/shard_map/ppermute | solution.py:31
  205.7 1.3 collective-permute-start.10
  207.6 4.3 %collective-permute-done.10 = f32[4,1,32,128]{3,2,1,0:T(8,128)S(1)} collective-permute-done((f32[4,1,32,128]{3,2,1,0:T(8,128)S(1)}, f32[4,1,32,128]{3,2,1,0:T(8,128)S(1)}, u32[]{:S(2)}, u32[]{:S(2)}) %collective-permute-start.10) | collective-permute-done | bytes 65568 | tf_op jit(solution)/shard_map/ppermute | solution.py:31
  (89 shorter events, 12.8 us)
Async XLA Ops:
  0.6 15.2 %collective-permute-start = (f32[4,1,2,128]{3,2,1,0:T(2,128)}, f32[4,1,2,128]{3,2,1,0:T(2,128)S(1)}, u32[]{:S(2)}, u32[]{:S(2)}) collective-permute-start(f32[4,1,2,128]{3,2,1,0:T(2,128)} %param.3), channel_id=1, source_target_pairs={{0,2},{1,3},{4,6},{5,7},{8,10},{9,11},{12,14},{13,15},{16,18},{17,... | collective-permute-start | bytes 12296 | tf_op jit(solution)/shard_map/ppermute | solution.py:19
  5.5 11.1 %collective-permute-start.1 = (f32[4,1,2,128]{3,2,1,0:T(2,128)}, f32[4,1,2,128]{3,2,1,0:T(2,128)S(1)}, u32[]{:S(2)}, u32[]{:S(2)}) collective-permute-start(f32[4,1,2,128]{3,2,1,0:T(2,128)} %param.3), channel_id=1, source_target_pairs={{2,0},{3,1},{6,4},{7,5},{10,8},{11,9},{14,12},{15,13},{18,16},{19,... | collective-permute-start | bytes 12296 | tf_op jit(solution)/shard_map/ppermute | solution.py:21
  6.8 132.0 %collective-permute-start.4 = (f32[4,1,32,128]{3,2,1,0:T(8,128)}, f32[4,1,32,128]{3,2,1,0:T(8,128)}, u32[]{:S(2)}, u32[]{:S(2)}) collective-permute-start(f32[4,1,32,128]{3,2,1,0:T(8,128)} %param.4), channel_id=1, source_target_pairs={{0,2},{1,3},{4,6},{5,7},{8,10},{9,11},{12,14},{13,15},{16,18},{17,... | collective-permute-start | bytes 196616 | tf_op jit(solution)/shard_map/ppermute | solution.py:19
  11.9 129.0 %collective-permute-start.5 = (f32[4,1,32,128]{3,2,1,0:T(8,128)}, f32[4,1,32,128]{3,2,1,0:T(8,128)S(1)}, u32[]{:S(2)}, u32[]{:S(2)}) collective-permute-start(f32[4,1,32,128]{3,2,1,0:T(8,128)} %param.4), channel_id=1, source_target_pairs={{2,0},{3,1},{6,4},{7,5},{10,8},{11,9},{14,12},{15,13},{18,16},{19,... | collective-permute-start | bytes 196616 | tf_op jit(solution)/shard_map/ppermute | solution.py:21
  15.8 46.8 %copy-start.11 = (s32[1024]{0:T(1024)}, s32[1024]{0:T(1024)S(1)}, u32[]{:S(2)}) copy-start(s32[1024]{0:T(1024)S(1)} %pad_clamp_fusion) | copy-start | bytes 12292
  16.6 9.3 %collective-permute-start.3 = (f32[4,3,2,128]{3,2,1,0:T(2,128)S(1)}, f32[4,3,2,128]{3,2,1,0:T(2,128)S(1)}, u32[]{:S(2)}, u32[]{:S(2)}) collective-permute-start(f32[4,3,2,128]{3,2,1,0:T(2,128)S(1)} %constant_dynamic-update-slice_fusion), channel_id=1, source_target_pairs={{0,4},{4,8},{8,12},{1,5},{5,9},{9,13},{2,6},{6,10},{10,14},{3,7},{... | collective-permute-start | bytes 36872 | tf_op jit(solution)/shard_map/ppermute | solution.py:31
  20.1 5.9 %collective-permute-start.2 = (f32[4,3,2,128]{3,2,1,0:T(2,128)S(1)}, f32[4,3,2,128]{3,2,1,0:T(2,128)S(1)}, u32[]{:S(2)}, u32[]{:S(2)}) collective-permute-start(f32[4,3,2,128]{3,2,1,0:T(2,128)S(1)} %constant_dynamic-update-slice_fusion), channel_id=1, source_target_pairs={{0,8},{4,12},{1,9},{5,13},{2,10},{6,14},{3,11},{7,15},{16,24},{20,... | collective-permute-start | bytes 36872 | tf_op jit(solution)/shard_map/ppermute | solution.py:31
  31.9 2.8 %copy-start = (f32[4,640,640]{2,1,0:T(8,128)}, f32[4,640,640]{2,1,0:T(8,128)S(1)}, u32[]{:S(2)}) copy-start(f32[4,640,640]{2,1,0:T(8,128)S(1)} %multiply_add_fusion) | copy-start | bytes 19660804
  62.6 2.0 copy-start.1
  86.5 53.8 %copy-start.10 = (f32[4,1,32,128]{3,2,1,0:T(8,128)S(1)}, f32[4,1,32,128]{3,2,1,0:T(8,128)}, u32[]{:S(2)}) copy-start(f32[4,1,32,128]{3,2,1,0:T(8,128)} %param.4) | copy-start | bytes 196612
  90.5 1.4 copy-start.2
  91.9 84.5 %copy-start.4 = (f32[4,128,128]{2,1,0:T(8,128)S(1)}, f32[4,128,128]{2,1,0:T(8,128)}, u32[]{:S(2)}) copy-start(f32[4,128,128]{2,1,0:T(8,128)} %get-tuple-element.7) | copy-start | bytes 786436
  91.9 86.3 %copy-start.5 = (f32[4,128,128]{2,1,0:T(8,128)S(1)}, f32[4,128,128]{2,1,0:T(8,128)}, u32[]{:S(2)}) copy-start(f32[4,128,128]{2,1,0:T(8,128)} %get-tuple-element.8) | copy-start | bytes 786436
  113.9 65.8 %copy-start.6 = (f32[4,128,128]{2,1,0:T(8,128)S(1)}, f32[4,128,128]{2,1,0:T(8,128)}, u32[]{:S(2)}) copy-start(f32[4,128,128]{2,1,0:T(8,128)} %get-tuple-element.9) | copy-start | bytes 786436
  116.2 1.0 copy-start.3
  141.5 29.4 %collective-permute-start.7 = (f32[4,3,32,128]{3,2,1,0:T(8,128)}, f32[4,3,32,128]{3,2,1,0:T(8,128)}, u32[]{:S(2)}, u32[]{:S(2)}) collective-permute-start(f32[4,3,32,128]{3,2,1,0:T(8,128)} %constant_dynamic-update-slice_fusion.3), channel_id=1, source_target_pairs={{0,4},{4,8},{8,12},{1,5},{5,9},{9,13},{2,6},{6,10},{10,14},{3,7},{... | collective-permute-start | bytes 589832 | tf_op jit(solution)/shard_map/ppermute | solution.py:31
  143.7 27.2 %collective-permute-start.6 = (f32[4,3,32,128]{3,2,1,0:T(8,128)}, f32[4,3,32,128]{3,2,1,0:T(8,128)}, u32[]{:S(2)}, u32[]{:S(2)}) collective-permute-start(f32[4,3,32,128]{3,2,1,0:T(8,128)} %constant_dynamic-update-slice_fusion.3), channel_id=1, source_target_pairs={{0,8},{4,12},{1,9},{5,13},{2,10},{6,14},{3,11},{7,15},{16,24},{20,... | collective-permute-start | bytes 589832 | tf_op jit(solution)/shard_map/ppermute | solution.py:31
  175.4 7.6 %copy-start.8 = (f32[4,128,128]{2,1,0:T(8,128)S(1)}, f32[4,128,128]{2,1,0:T(8,128)}, u32[]{:S(2)}) copy-start(f32[4,128,128]{2,1,0:T(8,128)} %get-tuple-element.11) | copy-start | bytes 786436
  175.4 8.8 %copy-start.7 = (f32[4,128,128]{2,1,0:T(8,128)S(1)}, f32[4,128,128]{2,1,0:T(8,128)}, u32[]{:S(2)}) copy-start(f32[4,128,128]{2,1,0:T(8,128)} %get-tuple-element.10) | copy-start | bytes 786436
  179.8 8.1 %copy-start.12 = (f32[20]{0:T(128)S(1)}, f32[20]{0:T(128)}, u32[]{:S(2)}) copy-start(f32[20]{0:T(128)} %mul.143) | copy-start | bytes 244
  179.8 8.1 %copy-start.13 = (s32[20]{0:T(128)S(1)}, s32[20]{0:T(128)}, u32[]{:S(2)}) copy-start(s32[20]{0:T(128)} %eq.25) | copy-start | bytes 244
  183.5 5.2 %copy-start.9 = (f32[4,128,32]{1,2,0:T(8,128)}, f32[4,128,32]{1,2,0:T(8,128)S(1)}, u32[]{:S(2)}) copy-start(f32[4,128,32]{1,2,0:T(8,128)S(1)} %fusion.54) | copy-start | bytes 196612
  188.8 12.4 %collective-permute-start.9 = (f32[4,3,32,128]{3,2,1,0:T(8,128)S(1)}, f32[4,3,32,128]{3,2,1,0:T(8,128)S(1)}, u32[]{:S(2)}, u32[]{:S(2)}) collective-permute-start(f32[4,3,32,128]{3,2,1,0:T(8,128)S(1)} %bitcast.109), channel_id=1, source_target_pairs={{8,0},{12,4},{9,1},{13,5},{10,2},{14,6},{11,3},{15,7},{24,16},{28,... | collective-permute-start | bytes 589832 | tf_op jit(solution)/shard_map/ppermute | solution.py:31
  190.1 11.0 %collective-permute-start.8 = (f32[4,3,32,128]{3,2,1,0:T(8,128)S(1)}, f32[4,3,32,128]{3,2,1,0:T(8,128)S(1)}, u32[]{:S(2)}, u32[]{:S(2)}) collective-permute-start(f32[4,3,32,128]{3,2,1,0:T(8,128)S(1)} %bitcast.110), channel_id=1, source_target_pairs={{4,0},{8,4},{12,8},{5,1},{9,5},{13,9},{6,2},{10,6},{14,10},{7,3},{... | collective-permute-start | bytes 589832 | tf_op jit(solution)/shard_map/ppermute | solution.py:31
  201.2 6.4 %collective-permute-start.11 = (f32[4,1,32,128]{3,2,1,0:T(8,128)S(1)}, f32[4,1,32,128]{3,2,1,0:T(8,128)S(1)}, u32[]{:S(2)}, u32[]{:S(2)}) collective-permute-start(f32[4,1,32,128]{3,2,1,0:T(8,128)S(1)} %get-tuple-element.24), channel_id=1, source_target_pairs={{0,2},{1,3},{4,6},{5,7},{8,10},{9,11},{12,14},{13,15},{16,18},{17,... | collective-permute-start | bytes 196616 | tf_op jit(solution)/shard_map/ppermute | solution.py:31
  205.7 6.2 %collective-permute-start.10 = (f32[4,1,32,128]{3,2,1,0:T(8,128)S(1)}, f32[4,1,32,128]{3,2,1,0:T(8,128)S(1)}, u32[]{:S(2)}, u32[]{:S(2)}) collective-permute-start(f32[4,1,32,128]{3,2,1,0:T(8,128)S(1)} %get-tuple-element.23), channel_id=1, source_target_pairs={{2,0},{3,1},{6,4},{7,5},{10,8},{11,9},{14,12},{15,13},{18,16},{19,... | collective-permute-start | bytes 196616 | tf_op jit(solution)/shard_map/ppermute | solution.py:31
where the time goes:
time: 217 us; the launch traced here: 213 us
  Pallas kernels  95.7 us (44%)
  starting transfers between devices  36.8 us (17%)
  matrix products  34 us (16%)
  local copies, waits for them, and re-layouts  18.6 us (9%)
  waiting for transfers between devices  14.5 us (7%)
  other arithmetic  11.6 us (5%)
    pallas_call x5, Pallas kernels, diag_factor(): return pl.pallas_call(_diag_kernel, out_shape=(shape, shape))(a)  95.7 us
    dot_general x26, matrix products, mm(): return jnp.einsum(spec, x, y, precision=lax.Precision.HIGHEST)  33.3 us
    ppermute x8, starting transfers between devices, shifted(): return lax.ppermute(block, axis, route)  24.3 us
    ppermute x8, waiting for transfers between devices, shifted(): return lax.ppermute(block, axis, route)  14.5 us
    unnamed x45, local copies, waits for them, and re-layouts  10.5 us
    ppermute x2, starting transfers between devices, padded_2(): lax.ppermute(tail, axis, [(i, (i + 1) % count) for i in range(ends)])  10 us
    add x1, other arithmetic, many_blocks(): mpts[:, :, None] * mpts[:, None, :] * kernel  5.3 us
  transfers between devices with their start and end apart: 12, of which 4 were waited for; matrix products, arithmetic and copies ran while one was open for 18% of the time, Pallas kernels for 45%

commit v1 on v0

--- a/solution.py
+++ b/solution.py
@@ -6,29 +6,6 @@
 
 ELL = 0.3
 NUGGET = 0.25
-
-
-def padded_2(cells, sides, width):
-    for axis, dim in sides:
-        count = lax.axis_size(axis)
-        ends = count - 1
-        head = lax.slice_in_dim(cells, 0, width, axis=dim)
-        tail = lax.slice_in_dim(cells, cells.shape[dim] - width, cells.shape[dim], axis=dim)
-        cells = jnp.concatenate(
-            [
-                lax.ppermute(tail, axis, [(i, (i + 1) % count) for i in range(ends)]),
-                cells,
-                lax.ppermute(head, axis, [((i + 1) % count, i) for i in range(ends)]),
-            ],
-            axis=dim,
-        )
-    return cells
-
-
-def shifted(block, axis, distance):
-    devices = range(lax.axis_size(axis))
-    route = [(i - distance, i) for i in devices if i - distance in devices]
-    return lax.ppermute(block, axis, route)
 
 
 def _diag_kernel(a_ref, u_ref, li_ref):
@@ -111,38 +88,44 @@
     return jnp.transpose(white, (0, 2, 1)), back
 
 
-def fetch_across(local):
-    return padded_2(local, (("grp", 1),), 1)
+def moved(block, blk_shift, grp_shift):
+    blks = lax.axis_size("blk")
+    grps = lax.axis_size("grp")
+    route = []
+    for b in range(blks):
+        for g in range(grps):
+            tb, tg = b + blk_shift, g + grp_shift
+            if 0 <= tb < blks and 0 <= tg < grps:
+                route.append((b * grps + g, tb * grps + tg))
+    return lax.ppermute(block, ("blk", "grp"), route)
 
 
-def fetch_older(local):
-    older = []
-    for distance in (2, 1):
-        older.append(shifted(local, "blk", distance))
-    return jnp.concatenate(older + [local], axis=0)
+def fetch_window(local):
+    rows = []
+    for back in (2, 1, 0):
+        row = []
+        for side in (-1, 0, 1):
+            row.append(local if back == 0 and side == 0 else moved(local, back, -side))
+        rows.append(jnp.concatenate(row, axis=1))
+    return jnp.concatenate(rows, axis=0)
 
 
-def back_across(terms):
-    total_count = terms[:, 1:2]
-    for column, offset in ((0, -1), (2, 1)):
-        total_count = total_count + shifted(terms[:, column : column + 1], "grp", offset)
-    return total_count
-
-
-def back_older(terms):
+def return_window(terms):
     per = terms.shape[0] // 3
-    farthest = terms[:per]
-    nearest = terms[per : 2 * per]
-    total_count = terms[2 * per :]
-    for distance, piece in ((1, nearest), (2, farthest)):
-        total_count = total_count + shifted(piece, "blk", -distance)
-    return total_count
+    total = terms[2 * per :, 1]
+    for index, back in enumerate((2, 1, 0)):
+        for column, side in enumerate((-1, 0, 1)):
+            if back == 0 and side == 0:
+                continue
+            piece = terms[index * per : (index + 1) * per, column]
+            total = total + moved(piece, -back, side)
+    return total[:, None]
 
 
 def per_device(coords, fields, neighbours):
     per = coords.shape[0]
-    window_coords = fetch_older(fetch_across(coords))
-    window_fields = fetch_older(fetch_across(fields))
+    window_coords = fetch_window(coords)
+    window_fields = fetch_window(fields)
     groups = lax.axis_size("grp")
     blk_pos = lax.axis_index("blk")
     grp_pos = lax.axis_index("grp")
@@ -170,7 +153,7 @@
         onehot, backs.reshape(width * per, local_fields * points), precision=lax.Precision.HIGHEST
     )
     terms = terms.reshape(3 * per, 3, local_fields, points)
-    product = back_across(back_older(terms))
+    product = return_window(terms)
     return (whitened[:, None], product)
 
 

time: 217 us -> 226 us (1.041)
  starting transfers between devices: 36.8 us -> 50.4 us
  local copies, waits for them, and re-layouts: 18.6 us -> 15.4 us
  waiting for transfers between devices: 14.5 us -> 11.9 us
    ppermute x12 -> x24, starting transfers between devices: 36.8 us -> 50.4 us  [moved(): return lax.ppermute(block, ('blk', 'grp'), route)]
    unnamed x45 -> x36, local copies, waits for them, and re-layouts: 10.5 us -> 7.89 us
    ppermute x12 -> x24, waiting for transfers between devices: 14.5 us -> 11.9 us  [moved(): return lax.ppermute(block, ('blk', 'grp'), route)]
  transfers between devices with their start and end apart: 12 -> 24, of which waited for: 4 -> 4; matrix products, arithmetic and copies ran while one was open for 18% -> 16% of each run, Pallas kernels for 45% -> 43%
where the time goes in v1:
time: 226 us; the launch traced here: 221 us
  Pallas kernels  95.8 us (42%)
  starting transfers between devices  50.4 us (22%)
  matrix products  34.2 us (15%)
  local copies, waits for them, and re-layouts  15.4 us (7%)
  other arithmetic  12.2 us (5%)
  waiting for transfers between devices  11.9 us (5%)
    pallas_call x5, Pallas kernels, diag_factor(): return pl.pallas_call(_diag_kernel, out_shape=(shape, shape))(a)  95.8 us
    ppermute x24, starting transfers between devices, moved(): return lax.ppermute(block, ('blk', 'grp'), route)  50.4 us
    dot_general x26, matrix products, mm(): return jnp.einsum(spec, x, y, precision=lax.Precision.HIGHEST)  33.3 us
    ppermute x24, waiting for transfers between devices, moved(): return lax.ppermute(block, ('blk', 'grp'), route)  11.9 us
    unnamed x36, local copies, waits for them, and re-layouts  7.89 us
    add x1, other arithmetic, many_blocks(): mpts[:, :, None] * mpts[:, None, :] * kernel  5.3 us
  transfers between devices with their start and end apart: 24, of which 4 were waited for; matrix products, arithmetic and copies ran while one was open for 16% of the time, Pallas kernels for 43%

profile of v1, /device:TPU:0, one launch (start us, length us, event | category | flops | bytes accessed | tf_op | source)
XLA Modules:
  0.0 221.4 jit_solution(6428889173399805470)
XLA Ops:
  0.6 1.3 collective-permute-start.7
  1.9 4.8 %collective-permute-start.6 = (f32[4,1,2,128]{3,2,1,0:T(2,128)}, f32[4,1,2,128]{3,2,1,0:T(2,128)S(1)}, u32[]{:S(2)}, u32[]{:S(2)}) collective-permute-start(f32[4,1,2,128]{3,2,1,0:T(2,128)} %param.3), channel_id=1, source_target_pairs={{0,2},{4,6},{8,10},{12,14},{1,3},{5,7},{9,11},{13,15},{16,18},{20,... | collective-permute-start | bytes 12296 | tf_op jit(solution)/shard_map/ppermute | solution.py:100
  7.5 5.3 %collective-permute-start.4 = (f32[4,1,2,128]{3,2,1,0:T(2,128)}, f32[4,1,2,128]{3,2,1,0:T(2,128)S(1)}, u32[]{:S(2)}, u32[]{:S(2)}) collective-permute-start(f32[4,1,2,128]{3,2,1,0:T(2,128)} %param.3), channel_id=1, source_target_pairs={{0,4},{2,6},{4,8},{6,10},{8,12},{10,14},{1,5},{3,7},{5,9},{7,11},{... | collective-permute-start | bytes 12296 | tf_op jit(solution)/shard_map/ppermute | solution.py:100
  12.7 6.6 %collective-permute-start.3 = (f32[4,1,2,128]{3,2,1,0:T(2,128)}, f32[4,1,2,128]{3,2,1,0:T(2,128)S(1)}, u32[]{:S(2)}, u32[]{:S(2)}) collective-permute-start(f32[4,1,2,128]{3,2,1,0:T(2,128)} %param.3), channel_id=1, source_target_pairs={{0,6},{4,10},{8,14},{1,7},{5,11},{9,15},{16,22},{20,26},{24,30},{1... | collective-permute-start | bytes 12296 | tf_op jit(solution)/shard_map/ppermute | solution.py:100
  23.2 1.3 collective-permute-start.1
  24.5 1.3 collective-permute-start
  27.1 1.3 collective-permute-start.15
  28.4 5.2 %collective-permute-start.14 = (f32[4,1,32,128]{3,2,1,0:T(8,128)}, f32[4,1,32,128]{3,2,1,0:T(8,128)}, u32[]{:S(2)}, u32[]{:S(2)}) collective-permute-start(f32[4,1,32,128]{3,2,1,0:T(8,128)} %param.4), channel_id=1, source_target_pairs={{0,2},{4,6},{8,10},{12,14},{1,3},{5,7},{9,11},{13,15},{16,18},{20,... | collective-permute-start | bytes 196616 | tf_op jit(solution)/shard_map/ppermute | solution.py:100
  33.6 1.3 collective-permute-start.13
  34.8 2.6 %collective-permute-start.12 = (f32[4,1,32,128]{3,2,1,0:T(8,128)}, f32[4,1,32,128]{3,2,1,0:T(8,128)}, u32[]{:S(2)}, u32[]{:S(2)}) collective-permute-start(f32[4,1,32,128]{3,2,1,0:T(8,128)} %param.4), channel_id=1, source_target_pairs={{0,4},{2,6},{4,8},{6,10},{8,12},{10,14},{1,5},{3,7},{5,9},{7,11},{... | collective-permute-start | bytes 196616 | tf_op jit(solution)/shard_map/ppermute | solution.py:100
  37.4 1.9 collective-permute-start.11
  40.7 5.3 %multiply_add_fusion = f32[4,640,640]{2,1,0:T(8,128)S(1)} fusion(f32[4,640]{1,0:T(4,128)S(1)} %get-tuple-element.18, f32[640,640]{1,0:T(8,128)S(1)} %fusion, f32[4,640]{1,0:T(4,128)S(1)} %get-tuple-element.30, f32[4,640]{1,0:T(4,128)S(1)} %get-tuple-element.31, f32[4,640]{1,0:T(4,128)S(1)} %get-tuple-element.19), kind=kLoop, calls=%fused_computation.2 | loop fusion | flops 21299200 | bytes 8232960 | tf_op jit(solution)/shard_map/add | solution.py:68
  46.0 2.7 %copy-done = f32[4,640,640]{2,1,0:T(8,128)} copy-done((f32[4,640,640]{2,1,0:T(8,128)}, f32[4,640,640]{2,1,0:T(8,128)S(1)}, u32[]{:S(2)}) %copy-start) | copy-done | bytes 6553624
  49.4 19.1 %shard_map.50 = (f32[4,128,128]{2,1,0:T(8,128)}, f32[4,128,128]{2,1,0:T(8,128)}) custom-call(f32[4,128,128]{2,1,0:T(8,128)} %slice.134.a_ref), custom_call_target="tpu_custom_call" | custom-call | tf_op jit(solution)/shard_map/pallas_call | solution.py:50
  68.5 2.3 %fusion.1 = f32[4,512,128]{2,1,0:T(8,128)S(1)} fusion(f32[4,128,128]{2,1,0:T(8,128)} %get-tuple-element.7, f32[4,640,640]{2,1,0:T(8,128)} %copy-done), kind=kOutput, calls=%fused_computation.18 | convolution fusion | flops 402653184 | bytes 2359296 | tf_op jit(solution)/shard_map/gic,gjc->gij/dot_general | solution.py:54
  70.9 5.7 %slice_subtract_fusion = f32[4,512,512]{2,1,0:T(8,128)S(1)} fusion(f32[4,640,640]{2,1,0:T(8,128)} %copy-done, f32[4,512,128]{2,1,0:T(8,128)S(1)} %fusion.1), kind=kOutput, calls=%fused_computation.3 | convolution fusion | flops 1611661312 | bytes 10485760 | tf_op jit(solution)/shard_map/gic,gjc->gij/dot_general | solution.py:54
  76.6 2.0 copy-done.1
  79.3 19.2 %shard_map.51 = (f32[4,128,128]{2,1,0:T(8,128)}, f32[4,128,128]{2,1,0:T(8,128)}) custom-call(f32[4,128,128]{2,1,0:T(8,128)} %slice.137.a_ref), custom_call_target="tpu_custom_call" | custom-call | tf_op jit(solution)/shard_map/pallas_call | solution.py:50
  98.5 2.0 fusion.3
  100.5 4.0 %slice_subtract_fusion.1 = f32[4,384,384]{2,1,0:T(8,128)S(1)} fusion(f32[4,512,512]{2,1,0:T(8,128)} %copy-done.1, f32[4,384,128]{2,1,0:T(8,128)S(1)} %fusion.3), kind=kOutput, calls=%fused_computation.4 | convolution fusion | flops 906559488 | bytes 6291456 | tf_op jit(solution)/shard_map/gic,gjc->gij/dot_general | solution.py:54
  104.6 1.4 copy-done.2
  106.7 19.1 %shard_map.52 = (f32[4,128,128]{2,1,0:T(8,128)}, f32[4,128,128]{2,1,0:T(8,128)}) custom-call(f32[4,128,128]{2,1,0:T(8,128)} %slice.140.a_ref), custom_call_target="tpu_custom_call" | custom-call | tf_op jit(solution)/shard_map/pallas_call | solution.py:50
  125.9 2.2 fusion.5
  128.0 2.2 %convolution_subtract_fusion = f32[4,256,256]{2,1,0:T(8,128)S(1)} fusion(f32[4,256,128]{2,1,0:T(8,128)S(1)} %fusion.5, f32[4,384,384]{2,1,0:T(8,128)} %copy-done.2), kind=kOutput, calls=%fused_computation.7 | convolution fusion | flops 402915328 | bytes 3145728 | tf_op jit(solution)/shard_map/gic,gjc->gij/dot_general | solution.py:54
  130.3 1.0 copy-done.3
  132.0 19.1 %shard_map.53 = (f32[4,128,128]{2,1,0:T(8,128)}, f32[4,128,128]{2,1,0:T(8,128)}) custom-call(f32[4,128,128]{2,1,0:T(8,128)} %slice.143.a_ref), custom_call_target="tpu_custom_call" | custom-call | tf_op jit(solution)/shard_map/pallas_call | solution.py:50
  151.2 1.7 fusion.10
  152.9 1.3 collective-permute-start.10
  154.2 1.9 collective-permute-start.9
  156.1 2.1 collective-permute-start.8
  158.1 2.3 %convolution_subtract_fusion.1.a_ref = f32[4,128,128]{2,1,0:T(8,128)} fusion(f32[4,128,128]{2,1,0:T(8,128)S(1)} %fusion.10, f32[4,256,256]{2,1,0:T(8,128)} %copy-done.3), kind=kOutput, calls=%fused_computation.8 | convolution fusion | flops 100728832 | bytes 1048576 | tf_op jit(solution)/shard_map/gic,gjc->gij/dot_general | solution.py:54
  160.5 19.2 %shard_map.54 = (f32[4,128,128]{2,1,0:T(8,128)}, f32[4,128,128]{2,1,0:T(8,128)}) custom-call(f32[4,128,128]{2,1,0:T(8,128)} %convolution_subtract_fusion.1.a_ref), custom_call_target="tpu_custom_call" | custom-call | tf_op jit(solution)/shard_map/pallas_call | solution.py:50
  179.6 1.9 maximum_maximum_fusion
  181.6 2.5 %gather_fusion.1 = f32[20,32,128]{2,1,0:T(8,128)} fusion(f32[36,32,128]{2,1,0:T(8,128)} %bitcast.138, s32[1024]{0:T(1024)} %copy-done.11), kind=kCustom, calls=%fused_computation.1 | custom fusion | bytes 655440 | tf_op jit(solution)/shard_map/gather | solution.py:147
  184.0 1.1 bitcast_multiply_fusion
  185.6 1.4 convolution_subtract_fusion.2
  187.6 1.0 convolution_subtract_fusion.3
  189.7 1.5 fusion.35
  196.4 0.9 fusion.7
  197.4 3.3 %collective-permute-start.23 = (f32[4,32,128]{2,0,1:T(4,128)S(1)}, f32[4,32,128]{2,0,1:T(4,128)S(1)}, u32[]{:S(2)}, u32[]{:S(2)}) collective-permute-start(f32[4,32,128]{2,0,1:T(4,128)S(1)} %get-tuple-element.21), channel_id=1, source_target_pairs={{0,2},{4,6},{8,10},{12,14},{1,3},{5,7},{9,11},{13,15},{16,18},{20,... | collective-permute-start | bytes 196616 | tf_op jit(solution)/shard_map/ppermute | solution.py:100
  200.8 1.3 collective-permute-start.22
  202.7 1.3 collective-permute-start.20
  204.0 1.3 collective-permute-start.19
  206.9 1.3 collective-permute-start.17
  208.2 1.3 collective-permute-start.16
  209.5 3.4 %collective-permute-done.20 = f32[4,32,128]{2,0,1:T(4,128)S(1)} collective-permute-done((f32[4,32,128]{2,0,1:T(4,128)S(1)}, f32[4,32,128]{2,0,1:T(4,128)S(1)}, u32[]{:S(2)}, u32[]{:S(2)}) %collective-permute-start.20) | collective-permute-done | bytes 65568 | tf_op jit(solution)/shard_map/ppermute | solution.py:100
  212.9 5.0 %collective-permute-done.17 = f32[4,32,128]{2,0,1:T(4,128)S(1)} collective-permute-done((f32[4,32,128]{2,0,1:T(4,128)S(1)}, f32[4,32,128]{2,0,1:T(4,128)S(1)}, u32[]{:S(2)}, u32[]{:S(2)}) %collective-permute-start.17) | collective-permute-done | bytes 65568 | tf_op jit(solution)/shard_map/ppermute | solution.py:100
  217.9 2.6 %collective-permute-done.16 = f32[4,32,128]{2,0,1:T(4,128)S(1)} collective-permute-done((f32[4,32,128]{2,0,1:T(4,128)S(1)}, f32[4,32,128]{2,0,1:T(4,128)S(1)}, u32[]{:S(2)}, u32[]{:S(2)}) %collective-permute-start.16) | collective-permute-done | bytes 65568 | tf_op jit(solution)/shard_map/ppermute | solution.py:100
  (102 shorter events, 20.4 us)
Async XLA Ops:
  0.6 21.9 %collective-permute-start.7 = (f32[4,1,2,128]{3,2,1,0:T(2,128)}, f32[4,1,2,128]{3,2,1,0:T(2,128)S(1)}, u32[]{:S(2)}, u32[]{:S(2)}) collective-permute-start(f32[4,1,2,128]{3,2,1,0:T(2,128)} %param.3), channel_id=1, source_target_pairs={{2,0},{6,4},{10,8},{14,12},{3,1},{7,5},{11,9},{15,13},{18,16},{22,... | collective-permute-start | bytes 12296 | tf_op jit(solution)/shard_map/ppermute | solution.py:100
  1.9 21.2 %collective-permute-start.6 = (f32[4,1,2,128]{3,2,1,0:T(2,128)}, f32[4,1,2,128]{3,2,1,0:T(2,128)S(1)}, u32[]{:S(2)}, u32[]{:S(2)}) collective-permute-start(f32[4,1,2,128]{3,2,1,0:T(2,128)} %param.3), channel_id=1, source_target_pairs={{0,2},{4,6},{8,10},{12,14},{1,3},{5,7},{9,11},{13,15},{16,18},{20,... | collective-permute-start | bytes 12296 | tf_op jit(solution)/shard_map/ppermute | solution.py:100
  6.8 17.7 %collective-permute-start.5 = (f32[4,1,2,128]{3,2,1,0:T(2,128)}, f32[4,1,2,128]{3,2,1,0:T(2,128)S(1)}, u32[]{:S(2)}, u32[]{:S(2)}) collective-permute-start(f32[4,1,2,128]{3,2,1,0:T(2,128)} %param.3), channel_id=1, source_target_pairs={{2,4},{6,8},{10,12},{3,5},{7,9},{11,13},{18,20},{22,24},{26,28},{1... | collective-permute-start | bytes 12296 | tf_op jit(solution)/shard_map/ppermute | solution.py:100
  7.5 19.6 %collective-permute-start.4 = (f32[4,1,2,128]{3,2,1,0:T(2,128)}, f32[4,1,2,128]{3,2,1,0:T(2,128)S(1)}, u32[]{:S(2)}, u32[]{:S(2)}) collective-permute-start(f32[4,1,2,128]{3,2,1,0:T(2,128)} %param.3), channel_id=1, source_target_pairs={{0,4},{2,6},{4,8},{6,10},{8,12},{10,14},{1,5},{3,7},{5,9},{7,11},{... | collective-permute-start | bytes 12296 | tf_op jit(solution)/shard_map/ppermute | solution.py:100
  12.7 15.6 %collective-permute-start.3 = (f32[4,1,2,128]{3,2,1,0:T(2,128)}, f32[4,1,2,128]{3,2,1,0:T(2,128)S(1)}, u32[]{:S(2)}, u32[]{:S(2)}) collective-permute-start(f32[4,1,2,128]{3,2,1,0:T(2,128)} %param.3), channel_id=1, source_target_pairs={{0,6},{4,10},{8,14},{1,7},{5,11},{9,15},{16,22},{20,26},{24,30},{1... | collective-permute-start | bytes 12296 | tf_op jit(solution)/shard_map/ppermute | solution.py:100
  22.5 18.1 %copy-start.11 = (s32[1024]{0:T(1024)}, s32[1024]{0:T(1024)S(1)}, u32[]{:S(2)}) copy-start(s32[1024]{0:T(1024)S(1)} %pad_clamp_fusion) | copy-start | bytes 12292
  22.5 11.1 %collective-permute-start.2 = (f32[4,1,2,128]{3,2,1,0:T(2,128)}, f32[4,1,2,128]{3,2,1,0:T(2,128)S(1)}, u32[]{:S(2)}, u32[]{:S(2)}) collective-permute-start(f32[4,1,2,128]{3,2,1,0:T(2,128)} %param.3), channel_id=1, source_target_pairs={{2,8},{6,12},{3,9},{7,13},{18,24},{22,28},{19,25},{23,29}} | collective-permute-start | bytes 12296 | tf_op jit(solution)/shard_map/ppermute | solution.py:100
  23.2 11.6 %collective-permute-start.1 = (f32[4,1,2,128]{3,2,1,0:T(2,128)}, f32[4,1,2,128]{3,2,1,0:T(2,128)S(1)}, u32[]{:S(2)}, u32[]{:S(2)}) collective-permute-start(f32[4,1,2,128]{3,2,1,0:T(2,128)} %param.3), channel_id=1, source_target_pairs={{0,8},{2,10},{4,12},{6,14},{1,9},{3,11},{5,13},{7,15},{16,24},{18,... | collective-permute-start | bytes 12296 | tf_op jit(solution)/shard_map/ppermute | solution.py:100
  24.5 12.9 %collective-permute-start = (f32[4,1,2,128]{3,2,1,0:T(2,128)}, f32[4,1,2,128]{3,2,1,0:T(2,128)S(1)}, u32[]{:S(2)}, u32[]{:S(2)}) collective-permute-start(f32[4,1,2,128]{3,2,1,0:T(2,128)} %param.3), channel_id=1, source_target_pairs={{0,10},{4,14},{1,11},{5,15},{16,26},{20,30},{17,27},{21,31}} | collective-permute-start | bytes 12296 | tf_op jit(solution)/shard_map/ppermute | solution.py:100
  27.1 125.8 %collective-permute-start.15 = (f32[4,1,32,128]{3,2,1,0:T(8,128)}, f32[4,1,32,128]{3,2,1,0:T(8,128)S(1)}, u32[]{:S(2)}, u32[]{:S(2)}) collective-permute-start(f32[4,1,32,128]{3,2,1,0:T(8,128)} %param.4), channel_id=1, source_target_pairs={{2,0},{6,4},{10,8},{14,12},{3,1},{7,5},{11,9},{15,13},{18,16},{22,... | collective-permute-start | bytes 196616 | tf_op jit(solution)/shard_map/ppermute | solution.py:100
  28.4 125.8 %collective-permute-start.14 = (f32[4,1,32,128]{3,2,1,0:T(8,128)}, f32[4,1,32,128]{3,2,1,0:T(8,128)}, u32[]{:S(2)}, u32[]{:S(2)}) collective-permute-start(f32[4,1,32,128]{3,2,1,0:T(8,128)} %param.4), channel_id=1, source_target_pairs={{0,2},{4,6},{8,10},{12,14},{1,3},{5,7},{9,11},{13,15},{16,18},{20,... | collective-permute-start | bytes 196616 | tf_op jit(solution)/shard_map/ppermute | solution.py:100
  33.6 122.5 %collective-permute-start.13 = (f32[4,1,32,128]{3,2,1,0:T(8,128)}, f32[4,1,32,128]{3,2,1,0:T(8,128)}, u32[]{:S(2)}, u32[]{:S(2)}) collective-permute-start(f32[4,1,32,128]{3,2,1,0:T(8,128)} %param.4), channel_id=1, source_target_pairs={{2,4},{6,8},{10,12},{3,5},{7,9},{11,13},{18,20},{22,24},{26,28},{1... | collective-permute-start | bytes 196616 | tf_op jit(solution)/shard_map/ppermute | solution.py:100
  34.8 144.8 %collective-permute-start.12 = (f32[4,1,32,128]{3,2,1,0:T(8,128)}, f32[4,1,32,128]{3,2,1,0:T(8,128)}, u32[]{:S(2)}, u32[]{:S(2)}) collective-permute-start(f32[4,1,32,128]{3,2,1,0:T(8,128)} %param.4), channel_id=1, source_target_pairs={{0,4},{2,6},{4,8},{6,10},{8,12},{10,14},{1,5},{3,7},{5,9},{7,11},{... | collective-permute-start | bytes 196616 | tf_op jit(solution)/shard_map/ppermute | solution.py:100
  37.4 142.2 %collective-permute-start.11 = (f32[4,1,32,128]{3,2,1,0:T(8,128)}, f32[4,1,32,128]{3,2,1,0:T(8,128)}, u32[]{:S(2)}, u32[]{:S(2)}) collective-permute-start(f32[4,1,32,128]{3,2,1,0:T(8,128)} %param.4), channel_id=1, source_target_pairs={{0,6},{4,10},{8,14},{1,7},{5,11},{9,15},{16,22},{20,26},{24,30},{1... | collective-permute-start | bytes 196616 | tf_op jit(solution)/shard_map/ppermute | solution.py:100
  46.0 2.7 %copy-start = (f32[4,640,640]{2,1,0:T(8,128)}, f32[4,640,640]{2,1,0:T(8,128)S(1)}, u32[]{:S(2)}) copy-start(f32[4,640,640]{2,1,0:T(8,128)S(1)} %multiply_add_fusion) | copy-start | bytes 19660804
  76.6 2.0 copy-start.1
  100.5 52.4 %copy-start.10 = (f32[4,1,32,128]{3,2,1,0:T(8,128)S(1)}, f32[4,1,32,128]{3,2,1,0:T(8,128)}, u32[]{:S(2)}) copy-start(f32[4,1,32,128]{3,2,1,0:T(8,128)} %param.4) | copy-start | bytes 196612
  104.6 1.4 copy-start.2
  106.0 79.1 %copy-start.4 = (f32[4,128,128]{2,1,0:T(8,128)S(1)}, f32[4,128,128]{2,1,0:T(8,128)}, u32[]{:S(2)}) copy-start(f32[4,128,128]{2,1,0:T(8,128)} %get-tuple-element.7) | copy-start | bytes 786436
  106.0 81.0 %copy-start.5 = (f32[4,128,128]{2,1,0:T(8,128)S(1)}, f32[4,128,128]{2,1,0:T(8,128)}, u32[]{:S(2)}) copy-start(f32[4,128,128]{2,1,0:T(8,128)} %get-tuple-element.8) | copy-start | bytes 786436
  125.9 62.6 %copy-start.6 = (f32[4,128,128]{2,1,0:T(8,128)S(1)}, f32[4,128,128]{2,1,0:T(8,128)}, u32[]{:S(2)}) copy-start(f32[4,128,128]{2,1,0:T(8,128)} %get-tuple-element.9) | copy-start | bytes 786436
  130.3 1.0 copy-start.3
  152.9 26.7 %collective-permute-start.10 = (f32[4,1,32,128]{3,2,1,0:T(8,128)S(1)}, f32[4,1,32,128]{3,2,1,0:T(8,128)}, u32[]{:S(2)}, u32[]{:S(2)}) collective-permute-start(f32[4,1,32,128]{3,2,1,0:T(8,128)S(1)} %copy-done.10), channel_id=1, source_target_pairs={{2,8},{6,12},{3,9},{7,13},{18,24},{22,28},{19,25},{23,29}} | collective-permute-start | bytes 196616 | tf_op jit(solution)/shard_map/ppermute | solution.py:100
  154.2 25.5 %collective-permute-start.9 = (f32[4,1,32,128]{3,2,1,0:T(8,128)S(1)}, f32[4,1,32,128]{3,2,1,0:T(8,128)}, u32[]{:S(2)}, u32[]{:S(2)}) collective-permute-start(f32[4,1,32,128]{3,2,1,0:T(8,128)S(1)} %copy-done.10), channel_id=1, source_target_pairs={{0,8},{2,10},{4,12},{6,14},{1,9},{3,11},{5,13},{7,15},{16,24},{18,... | collective-permute-start | bytes 196616 | tf_op jit(solution)/shard_map/ppermute | solution.py:100
  156.1 23.6 %collective-permute-start.8 = (f32[4,1,32,128]{3,2,1,0:T(8,128)S(1)}, f32[4,1,32,128]{3,2,1,0:T(8,128)}, u32[]{:S(2)}, u32[]{:S(2)}) collective-permute-start(f32[4,1,32,128]{3,2,1,0:T(8,128)S(1)} %copy-done.10), channel_id=1, source_target_pairs={{0,10},{4,14},{1,11},{5,15},{16,26},{20,30},{17,27},{21,31}} | collective-permute-start | bytes 196616 | tf_op jit(solution)/shard_map/ppermute | solution.py:100
  184.0 7.6 %copy-start.8 = (f32[4,128,128]{2,1,0:T(8,128)S(1)}, f32[4,128,128]{2,1,0:T(8,128)}, u32[]{:S(2)}) copy-start(f32[4,128,128]{2,1,0:T(8,128)} %get-tuple-element.11) | copy-start | bytes 786436
  184.0 8.9 %copy-start.7 = (f32[4,128,128]{2,1,0:T(8,128)S(1)}, f32[4,128,128]{2,1,0:T(8,128)}, u32[]{:S(2)}) copy-start(f32[4,128,128]{2,1,0:T(8,128)} %get-tuple-element.10) | copy-start | bytes 786436
  187.5 8.9 %copy-start.12 = (s32[12,3]{0,1:T(4,128)S(1)}, s32[12,3]{0,1:T(4,128)}, u32[]{:S(2)}) copy-start(s32[12,3]{0,1:T(4,128)} %multiply_add_fusion.1) | copy-start | bytes 436
  187.5 8.9 %copy-start.13 = (f32[20]{0:T(128)S(1)}, f32[20]{0:T(128)}, u32[]{:S(2)}) copy-start(f32[20]{0:T(128)} %mul.143) | copy-start | bytes 244
  187.5 8.9 %copy-start.14 = (s32[20]{0:T(128)S(1)}, s32[20]{0:T(128)}, u32[]{:S(2)}) copy-start(s32[20]{0:T(128)} %eq.36) | copy-start | bytes 244
  192.2 29.0 %copy-start.9 = (f32[4,128,32]{1,2,0:T(8,128)}, f32[4,128,32]{1,2,0:T(8,128)S(1)}, u32[]{:S(2)}) copy-start(f32[4,128,32]{1,2,0:T(8,128)S(1)} %fusion.65) | copy-start | bytes 196612
  197.4 7.9 %collective-permute-start.23 = (f32[4,32,128]{2,0,1:T(4,128)S(1)}, f32[4,32,128]{2,0,1:T(4,128)S(1)}, u32[]{:S(2)}, u32[]{:S(2)}) collective-permute-start(f32[4,32,128]{2,0,1:T(4,128)S(1)} %get-tuple-element.21), channel_id=1, source_target_pairs={{0,2},{4,6},{8,10},{12,14},{1,3},{5,7},{9,11},{13,15},{16,18},{20,... | collective-permute-start | bytes 196616 | tf_op jit(solution)/shard_map/ppermute | solution.py:100
  200.8 6.2 %collective-permute-start.22 = (f32[4,32,128]{2,0,1:T(4,128)S(1)}, f32[4,32,128]{2,0,1:T(4,128)S(1)}, u32[]{:S(2)}, u32[]{:S(2)}) collective-permute-start(f32[4,32,128]{2,0,1:T(4,128)S(1)} %get-tuple-element.22), channel_id=1, source_target_pairs={{2,0},{6,4},{10,8},{14,12},{3,1},{7,5},{11,9},{15,13},{18,16},{22,... | collective-permute-start | bytes 196616 | tf_op jit(solution)/shard_map/ppermute | solution.py:100
  202.1 6.2 %collective-permute-start.21 = (f32[4,32,128]{2,0,1:T(4,128)S(1)}, f32[4,32,128]{2,0,1:T(4,128)S(1)}, u32[]{:S(2)}, u32[]{:S(2)}) collective-permute-start(f32[4,32,128]{2,0,1:T(4,128)S(1)} %get-tuple-element.23), channel_id=1, source_target_pairs={{4,2},{8,6},{12,10},{5,3},{9,7},{13,11},{20,18},{24,22},{28,26},{2... | collective-permute-start | bytes 196616 | tf_op jit(solution)/shard_map/ppermute | solution.py:100
  202.7 10.2 %collective-permute-start.20 = (f32[4,32,128]{2,0,1:T(4,128)S(1)}, f32[4,32,128]{2,0,1:T(4,128)S(1)}, u32[]{:S(2)}, u32[]{:S(2)}) collective-permute-start(f32[4,32,128]{2,0,1:T(4,128)S(1)} %get-tuple-element.24), channel_id=1, source_target_pairs={{4,0},{6,2},{8,4},{10,6},{12,8},{14,10},{5,1},{7,3},{9,5},{11,7},{... | collective-permute-start | bytes 196616 | tf_op jit(solution)/shard_map/ppermute | solution.py:100
  204.0 8.9 %collective-permute-start.19 = (f32[4,32,128]{2,0,1:T(4,128)S(1)}, f32[4,32,128]{2,0,1:T(4,128)S(1)}, u32[]{:S(2)}, u32[]{:S(2)}) collective-permute-start(f32[4,32,128]{2,0,1:T(4,128)S(1)} %get-tuple-element.25), channel_id=1, source_target_pairs={{6,0},{10,4},{14,8},{7,1},{11,5},{15,9},{22,16},{26,20},{30,24},{2... | collective-permute-start | bytes 196616 | tf_op jit(solution)/shard_map/ppermute | solution.py:100
  205.3 7.6 %collective-permute-start.18 = (f32[4,32,128]{2,0,1:T(4,128)S(1)}, f32[4,32,128]{2,0,1:T(4,128)S(1)}, u32[]{:S(2)}, u32[]{:S(2)}) collective-permute-start(f32[4,32,128]{2,0,1:T(4,128)S(1)} %get-tuple-element.26), channel_id=1, source_target_pairs={{8,2},{12,6},{9,3},{13,7},{24,18},{28,22},{25,19},{29,23}} | collective-permute-start | bytes 196616 | tf_op jit(solution)/shard_map/ppermute | solution.py:100
  206.9 11.0 %collective-permute-start.17 = (f32[4,32,128]{2,0,1:T(4,128)S(1)}, f32[4,32,128]{2,0,1:T(4,128)S(1)}, u32[]{:S(2)}, u32[]{:S(2)}) collective-permute-start(f32[4,32,128]{2,0,1:T(4,128)S(1)} %get-tuple-element.27), channel_id=1, source_target_pairs={{8,0},{10,2},{12,4},{14,6},{9,1},{11,3},{13,5},{15,7},{24,16},{26,... | collective-permute-start | bytes 196616 | tf_op jit(solution)/shard_map/ppermute | solution.py:100
  208.2 12.3 %collective-permute-start.16 = (f32[4,32,128]{2,0,1:T(4,128)S(1)}, f32[4,32,128]{2,0,1:T(4,128)S(1)}, u32[]{:S(2)}, u32[]{:S(2)}) collective-permute-start(f32[4,32,128]{2,0,1:T(4,128)S(1)} %get-tuple-element.20), channel_id=1, source_target_pairs={{10,0},{14,4},{11,1},{15,5},{26,16},{30,20},{27,17},{31,21}} | collective-permute-start | bytes 196616 | tf_op jit(solution)/shard_map/ppermute | solution.py:100

commit v2 on v1

--- a/solution.py
+++ b/solution.py
@@ -88,73 +88,40 @@
     return jnp.transpose(white, (0, 2, 1)), back
 
 
-def moved(block, blk_shift, grp_shift):
-    blks = lax.axis_size("blk")
-    grps = lax.axis_size("grp")
-    route = []
-    for b in range(blks):
-        for g in range(grps):
-            tb, tg = b + blk_shift, g + grp_shift
-            if 0 <= tb < blks and 0 <= tg < grps:
-                route.append((b * grps + g, tb * grps + tg))
-    return lax.ppermute(block, ("blk", "grp"), route)
-
-
-def fetch_window(local):
-    rows = []
-    for back in (2, 1, 0):
-        row = []
-        for side in (-1, 0, 1):
-            row.append(local if back == 0 and side == 0 else moved(local, back, -side))
-        rows.append(jnp.concatenate(row, axis=1))
-    return jnp.concatenate(rows, axis=0)
-
-
-def return_window(terms):
-    per = terms.shape[0] // 3
-    total = terms[2 * per :, 1]
-    for index, back in enumerate((2, 1, 0)):
-        for column, side in enumerate((-1, 0, 1)):
-            if back == 0 and side == 0:
-                continue
-            piece = terms[index * per : (index + 1) * per, column]
-            total = total + moved(piece, -back, side)
-    return total[:, None]
-
-
 def per_device(coords, fields, neighbours):
     per = coords.shape[0]
-    window_coords = fetch_window(coords)
-    window_fields = fetch_window(fields)
     groups = lax.axis_size("grp")
+    blocks = lax.axis_size("blk") * groups * per
     blk_pos = lax.axis_index("blk")
     grp_pos = lax.axis_index("grp")
+    all_coords = lax.all_gather(coords[:, 0], ("blk", "grp"), axis=0, tiled=False)
+    all_fields = lax.all_gather(fields[:, 0], ("blk", "grp"), axis=0, tiled=False)
+    all_coords = all_coords.reshape((blocks,) + coords.shape[2:])
+    all_fields = all_fields.reshape((blocks,) + fields.shape[2:])
     neighbour_lists = neighbours.reshape(per, neighbours.shape[2])
-    earlier = neighbour_lists // groups - (blk_pos - 2) * per
-    beside = neighbour_lists % groups - grp_pos + 1
-    own_slot = ((2 * per + jnp.arange(per, dtype=jnp.int32)) * 3 + 1)[:, None]
-    slots = jnp.concatenate(
-        [jnp.where(neighbour_lists >= 0, earlier * 3 + beside, own_slot), own_slot], axis=1
+    own_ids = (blk_pos * per + jnp.arange(per, dtype=jnp.int32)) * groups + grp_pos
+    ids = jnp.concatenate(
+        [jnp.where(neighbour_lists >= 0, neighbour_lists, own_ids[:, None]), own_ids[:, None]], axis=1
     )
+    order = ids // groups
+    slots = (order // per * groups + ids % groups) * per + order % per
     masks = jnp.concatenate(
         [(neighbour_lists >= 0).astype(jnp.float32), jnp.ones((per, 1), jnp.float32)], axis=1
     )
-    flat_coords = window_coords.reshape((9 * per,) + coords.shape[2:])
-    flat_fields = window_fields.reshape((9 * per,) + fields.shape[2:])
     width = slots.shape[1]
     local_fields = fields.shape[2]
     points = fields.shape[3]
-    whitened, backs = many_blocks(flat_coords[slots], flat_fields[slots], masks)
-    onehot = (slots.reshape(-1)[None, :] == jnp.arange(9 * per, dtype=jnp.int32)[:, None]).astype(
+    whitened, backs = many_blocks(all_coords[slots], all_fields[slots], masks)
+    onehot = (slots.reshape(-1)[None, :] == jnp.arange(blocks, dtype=jnp.int32)[:, None]).astype(
         jnp.float32
     )
     onehot = onehot * masks.reshape(-1)[None, :]
     terms = jnp.dot(
         onehot, backs.reshape(width * per, local_fields * points), precision=lax.Precision.HIGHEST
     )
-    terms = terms.reshape(3 * per, 3, local_fields, points)
-    product = return_window(terms)
-    return (whitened[:, None], product)
+    terms = terms.reshape(blocks // per, per, local_fields, points)
+    product = lax.psum_scatter(terms, ("blk", "grp"), scatter_dimension=0, tiled=False)
+    return (whitened[:, None], product[:, None])
 
 
 def solution(mesh):

time: 226 us -> 304 us (1.35)
  blocking collectives: 0 us -> 65.7 us
  waiting for transfers between devices: 11.9 us -> 63.4 us
  starting transfers between devices: 50.4 us -> 0.04 us
  between operations: 1.46 us -> 14.5 us
  other arithmetic: 12.2 us -> 9 us
    all_gather x0 -> x2, blocking collectives: none -> 65.7 us  [the longest x1 33.4 us: per_device(): lax.all_gather(fields[:, 0], ('blk', 'grp'), axis=0, tiled=False)]
    reduce_scatter x0 -> x1, waiting for transfers between devices: none -> 63.4 us  [per_device(): lax.psum_scatter(terms, ('blk', 'grp'), scatter_dimension=0, tiled=False)]
    ppermute x24 -> x0, starting transfers between devices: 50.4 us -> none  [moved(): return lax.ppermute(block, ('blk', 'grp'), route)]
    ppermute x24 -> x0, waiting for transfers between devices: 11.9 us -> none  [moved(): return lax.ppermute(block, ('blk', 'grp'), route)]
    unnamed x36 -> x27, local copies, waits for them, and re-layouts: 7.89 us -> 7.16 us
  transfers between devices with their start and end apart: 24 -> 1, of which waited for: 4 -> 1; matrix products, arithmetic and copies ran while one was open for 16% -> 0% of each run, Pallas kernels for 43% -> 0%
where the time goes in v2:
time: 304 us; the launch traced here: 301 us
  Pallas kernels  95.7 us (31%)
  blocking collectives  65.7 us (22%)
  waiting for transfers between devices  63.4 us (21%)
  matrix products  34.1 us (11%)
  local copies, waits for them, and re-layouts  18.2 us (6%)
  between operations  14.5 us (5%)
  other arithmetic  9 us (3%)
    pallas_call x5, Pallas kernels, diag_factor(): return pl.pallas_call(_diag_kernel, out_shape=(shape, shape))(a)  95.7 us
    reduce_scatter x1, waiting for transfers between devices, per_device(): lax.psum_scatter(terms, ('blk', 'grp'), scatter_dimension=0, tiled=False)  63.4 us
    dot_general x26, matrix products, mm(): return jnp.einsum(spec, x, y, precision=lax.Precision.HIGHEST)  33.4 us
    all_gather x1, blocking collectives, per_device(): lax.all_gather(fields[:, 0], ('blk', 'grp'), axis=0, tiled=False)  33.4 us
    all_gather x1, blocking collectives, per_device(): lax.all_gather(coords[:, 0], ('blk', 'grp'), axis=0, tiled=False)  32.3 us
    unnamed x27, local copies, waits for them, and re-layouts  7.16 us
  transfers between devices with their start and end apart: 1, of which 1 were waited for; matrix products, arithmetic and copies ran while one was open for 0% of the time, Pallas kernels for 0%

profile of v2, /device:TPU:0, one launch (start us, length us, event | category | flops | bytes accessed | tf_op | source)
XLA Modules:
  0.0 300.7 jit_solution(5141266038877538458)
XLA Ops:
  7.4 0.7 broadcast_compare_fusion
  8.2 0.8 fusion.104
  9.0 0.8 broadcast_select_fusion
  9.7 32.3 %all-gather = f32[32,1,2,128]{3,2,1,0:T(2,128)S(1)} all-gather(f32[4,1,2,128]{3,2,1,0:T(2,128)} %param.3), channel_id=2, replica_groups=mesh['parts'=2,'blk'=4,'grp'=2,'fld'=2] {'blk','grp'}, dimensions={0}, use_global_device_ids=true | all-gather | bytes 36864 | tf_op jit(solution)/shard_map/all_gather | solution.py:97
  42.3 0.6 gather_fusion
  42.9 5.3 %multiply_add_fusion = f32[4,640,640]{2,1,0:T(8,128)S(1)} fusion(f32[4,640]{1,0:T(4,128)S(1)} %get-tuple-element.18, f32[640,640]{1,0:T(8,128)S(1)} %fusion, f32[4,640]{1,0:T(4,128)S(1)} %get-tuple-element.22, f32[4,640]{1,0:T(4,128)S(1)} %get-tuple-element.23, f32[4,640]{1,0:T(4,128)S(1)} %get-tuple-element.19), kind=kLoop, calls=%fused_computation.2 | loop fusion | flops 21299200 | bytes 8232960 | tf_op jit(solution)/shard_map/add | solution.py:68
  48.2 2.7 copy-done
  50.9 0.7 slice.98.a_ref
  51.7 19.2 %shard_map.50 = (f32[4,128,128]{2,1,0:T(8,128)}, f32[4,128,128]{2,1,0:T(8,128)}) custom-call(f32[4,128,128]{2,1,0:T(8,128)} %slice.98.a_ref), custom_call_target="tpu_custom_call" | custom-call | tf_op jit(solution)/shard_map/pallas_call | solution.py:50
  70.8 2.3 fusion.1
  73.1 5.7 %slice_subtract_fusion = f32[4,512,512]{2,1,0:T(8,128)S(1)} fusion(f32[4,640,640]{2,1,0:T(8,128)} %copy-done, f32[4,512,128]{2,1,0:T(8,128)S(1)} %fusion.1), kind=kOutput, calls=%fused_computation.3 | convolution fusion | flops 1611661312 | bytes 10485760 | tf_op jit(solution)/shard_map/gic,gjc->gij/dot_general | solution.py:54
  78.9 1.9 copy-done.1
  80.8 0.7 slice.101.a_ref
  81.6 19.1 %shard_map.51 = (f32[4,128,128]{2,1,0:T(8,128)}, f32[4,128,128]{2,1,0:T(8,128)}) custom-call(f32[4,128,128]{2,1,0:T(8,128)} %slice.101.a_ref), custom_call_target="tpu_custom_call" | custom-call | tf_op jit(solution)/shard_map/pallas_call | solution.py:50
  100.7 2.0 fusion.3
  102.7 4.0 %slice_subtract_fusion.1 = f32[4,384,384]{2,1,0:T(8,128)S(1)} fusion(f32[4,512,512]{2,1,0:T(8,128)} %copy-done.1, f32[4,384,128]{2,1,0:T(8,128)S(1)} %fusion.3), kind=kOutput, calls=%fused_computation.4 | convolution fusion | flops 906559488 | bytes 6291456 | tf_op jit(solution)/shard_map/gic,gjc->gij/dot_general | solution.py:54
  106.8 1.4 copy-done.2
  108.2 0.7 slice.104.a_ref
  108.9 19.1 %shard_map.52 = (f32[4,128,128]{2,1,0:T(8,128)}, f32[4,128,128]{2,1,0:T(8,128)}) custom-call(f32[4,128,128]{2,1,0:T(8,128)} %slice.104.a_ref), custom_call_target="tpu_custom_call" | custom-call | tf_op jit(solution)/shard_map/pallas_call | solution.py:50
  128.1 2.0 fusion.5
  130.1 2.3 convolution_subtract_fusion
  132.4 1.0 copy-done.3
  133.3 0.7 slice.107.a_ref
  134.1 19.1 %shard_map.53 = (f32[4,128,128]{2,1,0:T(8,128)}, f32[4,128,128]{2,1,0:T(8,128)}) custom-call(f32[4,128,128]{2,1,0:T(8,128)} %slice.107.a_ref), custom_call_target="tpu_custom_call" | custom-call | tf_op jit(solution)/shard_map/pallas_call | solution.py:50
  153.2 1.7 fusion.10
  154.9 2.7 convolution_subtract_fusion.1.a_ref
  157.6 19.2 %shard_map.54 = (f32[4,128,128]{2,1,0:T(8,128)}, f32[4,128,128]{2,1,0:T(8,128)}) custom-call(f32[4,128,128]{2,1,0:T(8,128)} %convolution_subtract_fusion.1.a_ref), custom_call_target="tpu_custom_call" | custom-call | tf_op jit(solution)/shard_map/pallas_call | solution.py:50
  176.8 33.4 %all-gather.1 = f32[32,1,32,128]{3,2,1,0:T(8,128)} all-gather(f32[4,1,32,128]{3,2,1,0:T(8,128)S(1)} %copy-done.10), channel_id=3, replica_groups=mesh['parts'=2,'blk'=4,'grp'=2,'fld'=2] {'blk','grp'}, dimensions={0}, use_global_device_ids=true | all-gather | bytes 589824 | tf_op jit(solution)/shard_map/all_gather | solution.py:98
  210.1 2.3 gather_fusion.1
  212.4 2.0 copy.41
  214.4 1.8 reshape.464
  216.3 1.1 broadcast_multiply_fusion
  217.3 0.5 fusion.33
  217.9 1.2 convolution_subtract_fusion.2
  219.0 0.5 fusion.31
  219.6 1.0 convolution_subtract_fusion.3
  220.5 0.5 fusion.29
  221.1 0.6 convolution_subtract_fusion.4
  221.7 1.5 fusion.27
  223.2 0.5 convolution_subtract_fusion.5
  223.7 0.5 fusion.58
  224.2 0.4 fusion.59
  225.3 0.4 convolution_negate_fusion.2
  226.0 0.6 convolution_negate_fusion.1
  227.0 0.7 convolution_negate_fusion
  228.6 0.7 fusion.7
  229.3 0.9 copy.22
  230.2 63.4 %reduce-scatter.2.cloned.1.call-done = f32[1,4,32,128]{3,2,1,0:T(8,128)} async-done(((f32[8,4,32,128]{3,2,1,0:T(8,128)}), f32[1,4,32,128]{3,2,1,0:T(8,128)}) %reduce-scatter.2.cloned.1.call-update) | async-done | bytes 65552 | tf_op jit(solution)/shard_map/reduce_scatter | solution.py:123
  (52 shorter events, 2.8 us)
Async XLA Ops:
  7.2 286.5 %reduce-scatter.2.cloned.1.call-start = ((), (), s32[]{:S(2)}) async-start(), calls=%async_computation.1 | async-start | bytes 589824 | tf_op jit(solution)/shard_map/reduce_scatter | solution.py:123
  48.2 2.7 copy-start
  78.9 2.0 copy-start.1
  102.7 74.0 %copy-start.10 = (f32[4,1,32,128]{3,2,1,0:T(8,128)S(1)}, f32[4,1,32,128]{3,2,1,0:T(8,128)}, u32[]{:S(2)}) copy-start(f32[4,1,32,128]{3,2,1,0:T(8,128)} %param.4) | copy-start | bytes 196612
  106.8 1.4 copy-start.2
  108.2 109.1 %copy-start.4 = (f32[4,128,128]{2,1,0:T(8,128)S(1)}, f32[4,128,128]{2,1,0:T(8,128)}, u32[]{:S(2)}) copy-start(f32[4,128,128]{2,1,0:T(8,128)} %get-tuple-element.7) | copy-start | bytes 786436
  128.1 91.0 %copy-start.5 = (f32[4,128,128]{2,1,0:T(8,128)S(1)}, f32[4,128,128]{2,1,0:T(8,128)}, u32[]{:S(2)}) copy-start(f32[4,128,128]{2,1,0:T(8,128)} %get-tuple-element.8) | copy-start | bytes 786436
  130.1 90.5 %copy-start.6 = (f32[4,128,128]{2,1,0:T(8,128)S(1)}, f32[4,128,128]{2,1,0:T(8,128)}, u32[]{:S(2)}) copy-start(f32[4,128,128]{2,1,0:T(8,128)} %get-tuple-element.9) | copy-start | bytes 786436
  132.4 1.0 copy-start.3
  216.3 7.4 %copy-start.8 = (f32[4,128,128]{2,1,0:T(8,128)S(1)}, f32[4,128,128]{2,1,0:T(8,128)}, u32[]{:S(2)}) copy-start(f32[4,128,128]{2,1,0:T(8,128)} %get-tuple-element.11) | copy-start | bytes 786436
  216.3 8.7 %copy-start.7 = (f32[4,128,128]{2,1,0:T(8,128)S(1)}, f32[4,128,128]{2,1,0:T(8,128)}, u32[]{:S(2)}) copy-start(f32[4,128,128]{2,1,0:T(8,128)} %get-tuple-element.10) | copy-start | bytes 786436
  224.2 69.4 %copy-start.9 = (f32[4,128,32]{1,2,0:T(8,128)}, f32[4,128,32]{1,2,0:T(8,128)S(1)}, u32[]{:S(2)}) copy-start(f32[4,128,32]{1,2,0:T(8,128)S(1)} %fusion.58) | copy-start | bytes 196612
Sparse Core Ops, SparseCore 0:
  230.4 63.2 reduce-scatter.1

commit v3 on v0

--- a/solution.py
+++ b/solution.py
@@ -3,6 +3,7 @@
 from jax import lax
 from jax.sharding import PartitionSpec as P
 from jax.experimental import pallas as pl
+from jax.experimental.pallas import tpu as pltpu
 
 ELL = 0.3
 NUGGET = 0.25
@@ -31,22 +32,24 @@
     return lax.ppermute(block, axis, route)
 
 
-def _diag_kernel(a_ref, u_ref, li_ref):
-    g_count, n, _ = a_ref.shape
+def _eliminate(a):
+    n = a.shape[0]
     rows = n // 8
     sub = lax.broadcasted_iota(jnp.int32, (8, n), 0)
     lane = lax.broadcasted_iota(jnp.int32, (8, n), 1)
-    lefts, rights, scales = [], [], []
-    for g in range(g_count):
-        lefts.append([a_ref[g, 8 * r : 8 * r + 8, :] for r in range(rows)])
-        rights.append(
-            [jnp.where(lane == sub + 8 * r, 1.0, 0.0).astype(jnp.float32) for r in range(rows)]
-        )
-        scales.append([jnp.zeros((8, n), jnp.float32) for r in range(rows)])
+    left = [a[8 * r : 8 * r + 8, :] for r in range(rows)]
+    right = [jnp.where(lane == sub + 8 * r, 1.0, 0.0).astype(jnp.float32) for r in range(rows)]
+    scale = [jnp.zeros((8, n), jnp.float32) for r in range(rows)]
+    return left, right, scale, sub
+
+
+def _eliminate_all(mats):
+    states = [_eliminate(a) for a in mats]
+    n = mats[0].shape[0]
+    rows = n // 8
     for j in range(n):
         r0, s = divmod(j, 8)
-        for g in range(g_count):
-            left, right, scale = lefts[g], rights[g], scales[g]
+        for left, right, scale, sub in states:
             row_l = jnp.broadcast_to(left[r0][s : s + 1, :], (8, n))
             row_r = jnp.broadcast_to(right[r0][s : s + 1, :], (8, n))
             piv = jnp.broadcast_to(row_l[:, j : j + 1], (8, n))
@@ -61,20 +64,79 @@
                     new_r = jnp.where(sub > s, new_r, right[r])
                 left[r] = new_l
                 right[r] = new_r
-    for g in range(g_count):
-        for r in range(rows):
-            upper = jnp.where(lane >= sub + 8 * r, lefts[g][r], 0.0)
-            u_ref[g, 8 * r : 8 * r + 8, :] = upper * scales[g][r]
-            li_ref[g, 8 * r : 8 * r + 8, :] = rights[g][r] * scales[g][r]
-
-
-def diag_factor(a):
-    shape = jax.ShapeDtypeStruct(a.shape, jnp.float32)
-    return pl.pallas_call(_diag_kernel, out_shape=(shape, shape))(a)
-
-
-def mm(spec, x, y):
-    return jnp.einsum(spec, x, y, precision=lax.Precision.HIGHEST)
+    return [
+        jnp.concatenate([right[r] * scale[r] for r in range(rows)], axis=0)
+        for left, right, scale, sub in states
+    ]
+
+
+def _dot(x, y, lhs_dim, rhs_dim):
+    return lax.dot_general(
+        x, y, (((lhs_dim,), (rhs_dim,)), ((), ())), precision=lax.Precision.HIGHEST,
+        preferred_element_type=jnp.float32,
+    )
+
+
+def _fused_kernel(cov_ref, val_ref, white_ref, back_ref, trail, panels, inverses, rest):
+    groups, slots, count, points = cov_ref.shape
+    trail[...] = cov_ref[...]
+    rest[...] = val_ref[...]
+    row_id = lax.broadcasted_iota(jnp.int32, (count, points), 0)
+
+    def forward(k, carry):
+        start = pl.multiple_of(k * points, points)
+        diag = [trail[g, k, pl.ds(start, points), :] for g in range(groups)]
+        invs = _eliminate_all(diag)
+        for g in range(groups):
+            inv = invs[g]
+            inverses[g, k] = inv
+            panel = _dot(trail[g, k], inv, 1, 1)
+            panel = jnp.where(row_id >= start + points, panel, 0.0)
+            panels[g, k] = panel
+            for c in range(slots):
+                trail[g, c] = trail[g, c] - _dot(panel, panel[c * points : (c + 1) * points], 1, 1)
+            white = _dot(inv, rest[g, pl.ds(start, points), :], 1, 0)
+            rest[g] = rest[g] - _dot(panel, white, 1, 0)
+            rest[g, pl.ds(start, points), :] = white
+        return carry
+
+    lax.fori_loop(0, slots, forward, 0)
+    last = (slots - 1) * points
+    for g in range(groups):
+        white = rest[g, last:, :]
+        white_ref[g] = white
+        back_ref[g] = jnp.zeros(back_ref.shape[1:], jnp.float32)
+        back_ref[g, last:, :] = _dot(inverses[g, slots - 1], white, 0, 0)
+
+    def backward(step, carry):
+        k = slots - 2 - step
+        start = pl.multiple_of(k * points, points)
+        for g in range(groups):
+            rhs = _dot(panels[g, k], back_ref[g], 0, 0)
+            back_ref[g, pl.ds(start, points), :] = -_dot(inverses[g, k], rhs, 0, 0)
+        return carry
+
+    lax.fori_loop(0, slots - 1, backward, 0)
+
+
+def fused_solve(cov_blocks, values):
+    groups, slots, count, points = cov_blocks.shape
+    fields = values.shape[2]
+    f32 = jnp.float32
+    return pl.pallas_call(
+        _fused_kernel,
+        out_shape=(
+            jax.ShapeDtypeStruct((groups, points, fields), f32),
+            jax.ShapeDtypeStruct((groups, count, fields), f32),
+        ),
+        scratch_shapes=[
+            pltpu.VMEM(cov_blocks.shape, f32),
+            pltpu.VMEM(cov_blocks.shape, f32),
+            pltpu.VMEM((groups, slots, points, points), f32),
+            pltpu.VMEM(values.shape, f32),
+        ],
+        compiler_params=pltpu.CompilerParams(vmem_limit_bytes=100 * 1024 * 1024),
+    )(cov_blocks, values)
 
 
 def many_blocks(pts, vals, mask):
@@ -89,23 +151,9 @@
     kernel = (1.0 + scaled) * jnp.exp(-scaled)
     eye = jnp.eye(count, dtype=jnp.float32)
     cov = mpts[:, :, None] * mpts[:, None, :] * kernel + eye * (NUGGET * mpts + 1.0 - mpts)[:, :, None]
+    cov_blocks = jnp.transpose(cov.reshape(groups, count, slots, points), (0, 2, 1, 3))
     values = jnp.transpose(vals, (0, 1, 3, 2)).reshape(groups, count, fields) * mpts[:, :, None]
-    trail = cov
-    rest = values
-    panels, inverses = [], []
-    for k in range(slots):
-        _, inv = diag_factor(trail[:, :points, :points])
-        inverses.append(inv)
-        white = mm("gij,gjf->gif", inv, rest[:, :points])
-        if k < slots - 1:
-            panel = mm("gic,gjc->gij", trail[:, points:, :points], inv)
-            panels.append(panel)
-            trail = trail[:, points:, points:] - mm("gic,gjc->gij", panel, panel)
-            rest = rest[:, points:] - mm("gic,gcf->gif", panel, white)
-    back = mm("gji,gjf->gif", inverses[-1], white)
-    for k in range(slots - 2, -1, -1):
-        rhs = -mm("gic,gif->gcf", panels[k], back)
-        back = jnp.concatenate([mm("gji,gjf->gif", inverses[k], rhs), back], axis=1)
+    white, back = fused_solve(cov_blocks, values)
     back = back * mpts[:, :, None]
     back = jnp.transpose(back.reshape(groups, slots, points, fields), (0, 1, 3, 2))
     return jnp.transpose(white, (0, 2, 1)), back

time: 217 us -> 238 us (1.097); the launches traced: 213 us -> 238 us
  Pallas kernels: 95.7 us -> 166 us
  matrix products: 34 us -> 1.32 us
  local copies, waits for them, and re-layouts: 18.6 us -> 6.25 us
  starting transfers between devices: 36.8 us -> 33.9 us
    pallas_call x5 -> x1, Pallas kernels: 95.7 us -> 166 us  [fused_solve(): pl.pallas_call(_fused_kernel, out_shape=(jax.ShapeDtypeStruct((groups, po...]
    dot_general x26 -> x0, matrix products: 33.3 us -> none  [mm(): return jnp.einsum(spec, x, y, precision=lax.Precision.HIGHEST)]
    unnamed x45 -> x19, local copies, waits for them, and re-layouts: 10.5 us -> 2.85 us
    slice x4 -> x0, local copies, waits for them, and re-layouts: 2.88 us -> none  [many_blocks(): _, inv = diag_factor(trail[:, :points, :points])]
  transfers between devices with their start and end apart: 12 -> 12, of which waited for: 4 -> 4; matrix products, arithmetic and copies ran while one was open for 18% -> 6% of each run, Pallas kernels for 45% -> 0%
where the time goes in v3:
time: 238 us
  Pallas kernels  166 us (70%)
  starting transfers between devices  33.9 us (14%)
  waiting for transfers between devices  16.2 us (7%)
  other arithmetic  12.9 us (5%)
  local copies, waits for them, and re-layouts  6.25 us (3%)
    pallas_call x1, Pallas kernels, fused_solve(): pl.pallas_call(_fused_kernel, out_shape=(jax.ShapeDtypeStruct((groups, po...  166 us
    ppermute x8, starting transfers between devices, shifted(): return lax.ppermute(block, axis, route)  21.9 us
    ppermute x8, waiting for transfers between devices, shifted(): return lax.ppermute(block, axis, route)  16.2 us
    ppermute x2, starting transfers between devices, padded_2(): lax.ppermute(tail, axis, [(i, (i + 1) % count) for i in range(ends)])  9.39 us
    add x1, other arithmetic, many_blocks(): mpts[:, :, None] * mpts[:, None, :] * kernel  6.41 us
  transfers between devices with their start and end apart: 12, of which 4 were waited for; matrix products, arithmetic and copies ran while one was open for 6% of the time, Pallas kernels for 0%

profile of v3, /device:TPU:0, one launch (start us, length us, event | category | flops | bytes accessed | tf_op | source)
XLA Modules:
  0.0 237.6 jit_solution(16313380364344243505)
XLA Ops:
  0.6 4.8 %collective-permute-start = (f32[4,1,2,128]{3,2,1,0:T(2,128)}, f32[4,1,2,128]{3,2,1,0:T(2,128)S(1)}, u32[]{:S(2)}, u32[]{:S(2)}) collective-permute-start(f32[4,1,2,128]{3,2,1,0:T(2,128)} %param.3), channel_id=1, source_target_pairs={{0,2},{1,3},{4,6},{5,7},{8,10},{9,11},{12,14},{13,15},{16,18},{17,... | collective-permute-start | bytes 12296 | tf_op jit(solution)/shard_map/ppermute | solution.py:20
  5.5 1.3 collective-permute-start.1
  6.8 4.5 %collective-permute-start.4 = (f32[4,1,32,128]{3,2,1,0:T(8,128)}, f32[4,1,32,128]{3,2,1,0:T(8,128)S(1)}, u32[]{:S(2)}, u32[]{:S(2)}) collective-permute-start(f32[4,1,32,128]{3,2,1,0:T(8,128)} %param.4), channel_id=1, source_target_pairs={{0,2},{1,3},{4,6},{5,7},{8,10},{9,11},{12,14},{13,15},{16,18},{17,... | collective-permute-start | bytes 196616 | tf_op jit(solution)/shard_map/ppermute | solution.py:20
  11.3 1.3 collective-permute-start.5
  12.7 0.7 broadcast_compare_fusion
  13.4 0.8 fusion.20
  14.1 0.8 fusion.10
  14.9 0.1 compare_select_fusion
  15.0 0.1 reshape.190
  15.1 0.1 broadcast_bitcast_fusion
  15.1 0.1 fusion
  15.3 0.7 constant_dynamic-update-slice_fusion.1
  16.0 0.0 collective-permute-done.1
  16.0 4.5 %collective-permute-start.2 = (f32[4,3,2,128]{3,2,1,0:T(2,128)S(1)}, f32[4,3,2,128]{3,2,1,0:T(2,128)S(1)}, u32[]{:S(2)}, u32[]{:S(2)}) collective-permute-start(f32[4,3,2,128]{3,2,1,0:T(2,128)S(1)} %constant_dynamic-update-slice_fusion), channel_id=1, source_target_pairs={{0,8},{4,12},{1,9},{5,13},{2,10},{6,14},{3,11},{7,15},{16,24},{20,... | collective-permute-start | bytes 36872 | tf_op jit(solution)/shard_map/ppermute | solution.py:32
  20.5 3.5 %collective-permute-start.3 = (f32[4,3,2,128]{3,2,1,0:T(2,128)S(1)}, f32[4,3,2,128]{3,2,1,0:T(2,128)S(1)}, u32[]{:S(2)}, u32[]{:S(2)}) collective-permute-start(f32[4,3,2,128]{3,2,1,0:T(2,128)S(1)} %constant_dynamic-update-slice_fusion), channel_id=1, source_target_pairs={{0,4},{4,8},{8,12},{1,5},{5,9},{9,13},{2,6},{6,10},{10,14},{3,7},{... | collective-permute-start | bytes 36872 | tf_op jit(solution)/shard_map/ppermute | solution.py:32
  24.0 0.1 pad_add_fusion
  24.1 0.6 mul.152
  24.7 0.6 eq.26
  25.3 0.0 collective-permute-done.2
  25.3 0.1 collective-permute-done.3
  25.4 0.6 gather_fusion
  26.0 0.1 slice_reduce_fusion.1
  26.1 0.0 collective-permute-done.4
  26.1 0.8 constant_dynamic-update-slice_fusion.4
  27.0 3.7 %collective-permute-start.6 = (f32[4,3,32,128]{3,2,1,0:T(8,128)S(1)}, f32[4,3,32,128]{3,2,1,0:T(8,128)S(1)}, u32[]{:S(2)}, u32[]{:S(2)}) collective-permute-start(f32[4,3,32,128]{3,2,1,0:T(8,128)S(1)} %constant_dynamic-update-slice_fusion.3), channel_id=1, source_target_pairs={{0,8},{4,12},{1,9},{5,13},{2,10},{6,14},{3,11},{7,15},{16,24},{20,... | collective-permute-start | bytes 589832 | tf_op jit(solution)/shard_map/ppermute | solution.py:32
  30.7 1.9 collective-permute-start.7
  32.5 6.4 %multiply_add_fusion.cov_ref = f32[4,5,640,128]{3,2,1,0:T(8,128)} fusion(f32[4,640]{1,0:T(4,128)S(1)} %get-tuple-element.14, f32[5,640,128]{2,1,0:T(8,128)S(1)} %fusion, f32[4,5,128]{2,1,0:T(8,128)S(1)} %sub.101, f32[4,640]{1,0:T(4,128)S(1)} %get-tuple-element.23, f32[4,5,128]{2,1,0:T(8,128)S(1)} %sub.96, f32[4,640]{1,0:T(4,128)S(1)} %get-tuple-element.24, ...), kind=kLoop, calls=%fused_computation.2 | loop fusion | flops 21299200 | bytes 8253520 | tf_op jit(solution)/shard_map/add | solution.py:153
  39.0 0.6 gather_fusion.1
  39.6 0.4 copy.14
  40.0 1.5 broadcast_multiply_fusion.1.val_ref
  41.4 166.1 %shard_map.50 = (f32[4,128,32]{2,1,0:T(8,128)}, f32[4,640,32]{2,1,0:T(8,128)}) custom-call(f32[4,5,640,128]{3,2,1,0:T(8,128)} %multiply_add_fusion.cov_ref, f32[4,640,32]{2,1,0:T(8,128)} %broadcast_multiply_fusion.1.val_ref), custom_call_target="tpu_custom_call" | custom-call | tf_op jit(solution)/shard_map/pallas_call | solution.py:126
  207.6 1.8 broadcast_multiply_fusion
  209.3 0.4 copy.15
  209.8 0.2 copy.20
  210.0 1.3 fusion.2
  211.3 0.1 fusion.17
  211.4 0.1 copy.22
  211.5 1.3 collective-permute-start.8
  212.8 0.1 copy.23
  212.9 1.3 collective-permute-start.9
  214.2 0.1 copy.21
  214.2 5.9 %collective-permute-done.8 = f32[4,3,32,128]{3,2,1,0:T(8,128)S(1)} collective-permute-done((f32[4,3,32,128]{3,2,1,0:T(8,128)S(1)}, f32[4,3,32,128]{3,2,1,0:T(8,128)S(1)}, u32[]{:S(2)}, u32[]{:S(2)}) %collective-permute-start.8) | collective-permute-done | bytes 196640 | tf_op jit(solution)/shard_map/ppermute | solution.py:32
  220.1 9.1 %collective-permute-done.9 = f32[4,3,32,128]{3,2,1,0:T(8,128)S(1)} collective-permute-done((f32[4,3,32,128]{3,2,1,0:T(8,128)S(1)}, f32[4,3,32,128]{3,2,1,0:T(8,128)S(1)}, u32[]{:S(2)}, u32[]{:S(2)}) %collective-permute-start.9) | collective-permute-done | bytes 196640 | tf_op jit(solution)/shard_map/ppermute | solution.py:32
  229.3 1.3 collective-permute-start.10
  230.6 4.5 %collective-permute-start.11 = (f32[4,1,32,128]{3,2,1,0:T(8,128)S(1)}, f32[4,1,32,128]{3,2,1,0:T(8,128)S(1)}, u32[]{:S(2)}, u32[]{:S(2)}) collective-permute-start(f32[4,1,32,128]{3,2,1,0:T(8,128)S(1)} %get-tuple-element.20), channel_id=1, source_target_pairs={{0,2},{1,3},{4,6},{5,7},{8,10},{9,11},{12,14},{13,15},{16,18},{17,... | collective-permute-start | bytes 196616 | tf_op jit(solution)/shard_map/ppermute | solution.py:32
  235.1 0.7 copy.16
  235.9 1.1 collective-permute-done.11
  237.0 0.6 fusion.1
  (31 shorter events, 0.3 us)
Async XLA Ops:
  0.6 14.7 %collective-permute-start = (f32[4,1,2,128]{3,2,1,0:T(2,128)}, f32[4,1,2,128]{3,2,1,0:T(2,128)S(1)}, u32[]{:S(2)}, u32[]{:S(2)}) collective-permute-start(f32[4,1,2,128]{3,2,1,0:T(2,128)} %param.3), channel_id=1, source_target_pairs={{0,2},{1,3},{4,6},{5,7},{8,10},{9,11},{12,14},{13,15},{16,18},{17,... | collective-permute-start | bytes 12296 | tf_op jit(solution)/shard_map/ppermute | solution.py:20
  5.5 10.5 %collective-permute-start.1 = (f32[4,1,2,128]{3,2,1,0:T(2,128)}, f32[4,1,2,128]{3,2,1,0:T(2,128)S(1)}, u32[]{:S(2)}, u32[]{:S(2)}) collective-permute-start(f32[4,1,2,128]{3,2,1,0:T(2,128)} %param.3), channel_id=1, source_target_pairs={{2,0},{3,1},{6,4},{7,5},{10,8},{11,9},{14,12},{15,13},{18,16},{19,... | collective-permute-start | bytes 12296 | tf_op jit(solution)/shard_map/ppermute | solution.py:22
  6.8 19.3 %collective-permute-start.4 = (f32[4,1,32,128]{3,2,1,0:T(8,128)}, f32[4,1,32,128]{3,2,1,0:T(8,128)S(1)}, u32[]{:S(2)}, u32[]{:S(2)}) collective-permute-start(f32[4,1,32,128]{3,2,1,0:T(8,128)} %param.4), channel_id=1, source_target_pairs={{0,2},{1,3},{4,6},{5,7},{8,10},{9,11},{12,14},{13,15},{16,18},{17,... | collective-permute-start | bytes 196616 | tf_op jit(solution)/shard_map/ppermute | solution.py:20
  11.3 15.6 %collective-permute-start.5 = (f32[4,1,32,128]{3,2,1,0:T(8,128)}, f32[4,1,32,128]{3,2,1,0:T(8,128)S(1)}, u32[]{:S(2)}, u32[]{:S(2)}) collective-permute-start(f32[4,1,32,128]{3,2,1,0:T(8,128)} %param.4), channel_id=1, source_target_pairs={{2,0},{3,1},{6,4},{7,5},{10,8},{11,9},{14,12},{15,13},{18,16},{19,... | collective-permute-start | bytes 196616 | tf_op jit(solution)/shard_map/ppermute | solution.py:22
  15.1 24.8 %copy-start.1 = (f32[4,640]{1,0:T(4,128)}, f32[4,640]{1,0:T(4,128)S(1)}, u32[]{:S(2)}) copy-start(f32[4,640]{1,0:T(4,128)S(1)} %get-tuple-element.15) | copy-start | bytes 30724
  16.0 9.3 %collective-permute-start.2 = (f32[4,3,2,128]{3,2,1,0:T(2,128)S(1)}, f32[4,3,2,128]{3,2,1,0:T(2,128)S(1)}, u32[]{:S(2)}, u32[]{:S(2)}) collective-permute-start(f32[4,3,2,128]{3,2,1,0:T(2,128)S(1)} %constant_dynamic-update-slice_fusion), channel_id=1, source_target_pairs={{0,8},{4,12},{1,9},{5,13},{2,10},{6,14},{3,11},{7,15},{16,24},{20,... | collective-permute-start | bytes 36872 | tf_op jit(solution)/shard_map/ppermute | solution.py:32
  20.5 4.9 %collective-permute-start.3 = (f32[4,3,2,128]{3,2,1,0:T(2,128)S(1)}, f32[4,3,2,128]{3,2,1,0:T(2,128)S(1)}, u32[]{:S(2)}, u32[]{:S(2)}) collective-permute-start(f32[4,3,2,128]{3,2,1,0:T(2,128)S(1)} %constant_dynamic-update-slice_fusion), channel_id=1, source_target_pairs={{0,4},{4,8},{8,12},{1,5},{5,9},{9,13},{2,6},{6,10},{10,14},{3,7},{... | collective-permute-start | bytes 36872 | tf_op jit(solution)/shard_map/ppermute | solution.py:32
  27.0 11.9 %collective-permute-start.6 = (f32[4,3,32,128]{3,2,1,0:T(8,128)S(1)}, f32[4,3,32,128]{3,2,1,0:T(8,128)S(1)}, u32[]{:S(2)}, u32[]{:S(2)}) collective-permute-start(f32[4,3,32,128]{3,2,1,0:T(8,128)S(1)} %constant_dynamic-update-slice_fusion.3), channel_id=1, source_target_pairs={{0,8},{4,12},{1,9},{5,13},{2,10},{6,14},{3,11},{7,15},{16,24},{20,... | collective-permute-start | bytes 589832 | tf_op jit(solution)/shard_map/ppermute | solution.py:32
  30.7 8.3 %collective-permute-start.7 = (f32[4,3,32,128]{3,2,1,0:T(8,128)S(1)}, f32[4,3,32,128]{3,2,1,0:T(8,128)S(1)}, u32[]{:S(2)}, u32[]{:S(2)}) collective-permute-start(f32[4,3,32,128]{3,2,1,0:T(8,128)S(1)} %constant_dynamic-update-slice_fusion.3), channel_id=1, source_target_pairs={{0,4},{4,8},{8,12},{1,5},{5,9},{9,13},{2,6},{6,10},{10,14},{3,7},{... | collective-permute-start | bytes 589832 | tf_op jit(solution)/shard_map/ppermute | solution.py:32
  207.6 27.5 %copy-start = (f32[4,128,32]{2,1,0:T(8,128)S(1)}, f32[4,128,32]{2,1,0:T(8,128)}, u32[]{:S(2)}) copy-start(f32[4,128,32]{2,1,0:T(8,128)} %get-tuple-element.4) | copy-start | bytes 196612
  211.5 8.6 %collective-permute-start.8 = (f32[4,3,32,128]{3,2,1,0:T(8,128)S(1)}, f32[4,3,32,128]{3,2,1,0:T(8,128)S(1)}, u32[]{:S(2)}, u32[]{:S(2)}) collective-permute-start(f32[4,3,32,128]{3,2,1,0:T(8,128)S(1)} %bitcast.64), channel_id=1, source_target_pairs={{4,0},{8,4},{12,8},{5,1},{9,5},{13,9},{6,2},{10,6},{14,10},{7,3},{... | collective-permute-start | bytes 589832 | tf_op jit(solution)/shard_map/ppermute | solution.py:32
  212.9 16.3 %collective-permute-start.9 = (f32[4,3,32,128]{3,2,1,0:T(8,128)S(1)}, f32[4,3,32,128]{3,2,1,0:T(8,128)S(1)}, u32[]{:S(2)}, u32[]{:S(2)}) collective-permute-start(f32[4,3,32,128]{3,2,1,0:T(8,128)S(1)} %bitcast.65), channel_id=1, source_target_pairs={{8,0},{12,4},{9,1},{13,5},{10,2},{14,6},{11,3},{15,7},{24,16},{28,... | collective-permute-start | bytes 589832 | tf_op jit(solution)/shard_map/ppermute | solution.py:32
  229.3 6.6 %collective-permute-start.10 = (f32[4,1,32,128]{3,2,1,0:T(8,128)S(1)}, f32[4,1,32,128]{3,2,1,0:T(8,128)S(1)}, u32[]{:S(2)}, u32[]{:S(2)}) collective-permute-start(f32[4,1,32,128]{3,2,1,0:T(8,128)S(1)} %get-tuple-element.19), channel_id=1, source_target_pairs={{2,0},{3,1},{6,4},{7,5},{10,8},{11,9},{14,12},{15,13},{18,16},{19,... | collective-permute-start | bytes 196616 | tf_op jit(solution)/shard_map/ppermute | solution.py:32
  230.6 6.4 %collective-permute-start.11 = (f32[4,1,32,128]{3,2,1,0:T(8,128)S(1)}, f32[4,1,32,128]{3,2,1,0:T(8,128)S(1)}, u32[]{:S(2)}, u32[]{:S(2)}) collective-permute-start(f32[4,1,32,128]{3,2,1,0:T(8,128)S(1)} %get-tuple-element.20), channel_id=1, source_target_pairs={{0,2},{1,3},{4,6},{5,7},{8,10},{9,11},{12,14},{13,15},{16,18},{17,... | collective-permute-start | bytes 196616 | tf_op jit(solution)/shard_map/ppermute | solution.py:32

commit v4 on v3

--- a/solution.py
+++ b/solution.py
@@ -93,8 +93,13 @@
             panel = _dot(trail[g, k], inv, 1, 1)
             panel = jnp.where(row_id >= start + points, panel, 0.0)
             panels[g, k] = panel
-            for c in range(slots):
-                trail[g, c] = trail[g, c] - _dot(panel, panel[c * points : (c + 1) * points], 1, 1)
+
+            def update(c, carry, g=g):
+                lower = panels[g, k, pl.ds(pl.multiple_of(c * points, points), points), :]
+                trail[g, c] = trail[g, c] - _dot(panels[g, k], lower, 1, 1)
+                return carry
+
+            lax.fori_loop(k + 1, slots, update, 0)
             white = _dot(inv, rest[g, pl.ds(start, points), :], 1, 0)
             rest[g] = rest[g] - _dot(panel, white, 1, 0)
             rest[g, pl.ds(start, points), :] = white

time: 238 us -> 221 us (0.929)
  Pallas kernels: 166 us -> 148 us
    pallas_call x1, Pallas kernels: 166 us -> 148 us  [fused_solve(): pl.pallas_call(_fused_kernel, out_shape=(jax.ShapeDtypeStruct((groups, po...]
where the time goes in v4:
time: 221 us; the launch traced here: 220 us
  Pallas kernels  148 us (67%)
  starting transfers between devices  33.9 us (15%)
  waiting for transfers between devices  16.2 us (7%)
  other arithmetic  12.9 us (6%)
  local copies, waits for them, and re-layouts  6.25 us (3%)
    pallas_call x1, Pallas kernels, fused_solve(): pl.pallas_call(_fused_kernel, out_shape=(jax.ShapeDtypeStruct((groups, po...  148 us
    ppermute x8, starting transfers between devices, shifted(): return lax.ppermute(block, axis, route)  21.9 us
    ppermute x8, waiting for transfers between devices, shifted(): return lax.ppermute(block, axis, route)  16.2 us
    ppermute x2, starting transfers between devices, padded_2(): lax.ppermute(tail, axis, [(i, (i + 1) % count) for i in range(ends)])  9.39 us
    add x1, other arithmetic, many_blocks(): mpts[:, :, None] * mpts[:, None, :] * kernel  6.41 us
  transfers between devices with their start and end apart: 12, of which 4 were waited for; matrix products, arithmetic and copies ran while one was open for 6% of the time, Pallas kernels for 0%

profile of v4, /device:TPU:0, one launch (start us, length us, event | category | flops | bytes accessed | tf_op | source)
XLA Modules:
  0.0 220.0 jit_solution(3377387990870275878)
XLA Ops:
  0.6 4.8 %collective-permute-start = (f32[4,1,2,128]{3,2,1,0:T(2,128)}, f32[4,1,2,128]{3,2,1,0:T(2,128)S(1)}, u32[]{:S(2)}, u32[]{:S(2)}) collective-permute-start(f32[4,1,2,128]{3,2,1,0:T(2,128)} %param.3), channel_id=1, source_target_pairs={{0,2},{1,3},{4,6},{5,7},{8,10},{9,11},{12,14},{13,15},{16,18},{17,... | collective-permute-start | bytes 12296 | tf_op jit(solution)/shard_map/ppermute | solution.py:20
  5.5 1.3 collective-permute-start.1
  6.8 4.5 %collective-permute-start.4 = (f32[4,1,32,128]{3,2,1,0:T(8,128)}, f32[4,1,32,128]{3,2,1,0:T(8,128)S(1)}, u32[]{:S(2)}, u32[]{:S(2)}) collective-permute-start(f32[4,1,32,128]{3,2,1,0:T(8,128)} %param.4), channel_id=1, source_target_pairs={{0,2},{1,3},{4,6},{5,7},{8,10},{9,11},{12,14},{13,15},{16,18},{17,... | collective-permute-start | bytes 196616 | tf_op jit(solution)/shard_map/ppermute | solution.py:20
  11.3 1.3 collective-permute-start.5
  12.7 0.7 broadcast_compare_fusion
  13.4 0.8 fusion.20
  14.1 0.8 fusion.10
  14.9 0.1 compare_select_fusion
  15.0 0.1 reshape.190
  15.1 0.1 broadcast_bitcast_fusion
  15.1 0.1 fusion
  15.3 0.7 constant_dynamic-update-slice_fusion.1
  16.0 0.0 collective-permute-done.1
  16.0 4.5 %collective-permute-start.2 = (f32[4,3,2,128]{3,2,1,0:T(2,128)S(1)}, f32[4,3,2,128]{3,2,1,0:T(2,128)S(1)}, u32[]{:S(2)}, u32[]{:S(2)}) collective-permute-start(f32[4,3,2,128]{3,2,1,0:T(2,128)S(1)} %constant_dynamic-update-slice_fusion), channel_id=1, source_target_pairs={{0,8},{4,12},{1,9},{5,13},{2,10},{6,14},{3,11},{7,15},{16,24},{20,... | collective-permute-start | bytes 36872 | tf_op jit(solution)/shard_map/ppermute | solution.py:32
  20.5 3.5 %collective-permute-start.3 = (f32[4,3,2,128]{3,2,1,0:T(2,128)S(1)}, f32[4,3,2,128]{3,2,1,0:T(2,128)S(1)}, u32[]{:S(2)}, u32[]{:S(2)}) collective-permute-start(f32[4,3,2,128]{3,2,1,0:T(2,128)S(1)} %constant_dynamic-update-slice_fusion), channel_id=1, source_target_pairs={{0,4},{4,8},{8,12},{1,5},{5,9},{9,13},{2,6},{6,10},{10,14},{3,7},{... | collective-permute-start | bytes 36872 | tf_op jit(solution)/shard_map/ppermute | solution.py:32
  24.0 0.1 pad_add_fusion
  24.1 0.6 mul.152
  24.7 0.6 eq.26
  25.3 0.0 collective-permute-done.2
  25.3 0.1 collective-permute-done.3
  25.4 0.6 gather_fusion
  26.0 0.1 slice_reduce_fusion.1
  26.1 0.0 collective-permute-done.4
  26.1 0.8 constant_dynamic-update-slice_fusion.4
  27.0 3.7 %collective-permute-start.6 = (f32[4,3,32,128]{3,2,1,0:T(8,128)S(1)}, f32[4,3,32,128]{3,2,1,0:T(8,128)S(1)}, u32[]{:S(2)}, u32[]{:S(2)}) collective-permute-start(f32[4,3,32,128]{3,2,1,0:T(8,128)S(1)} %constant_dynamic-update-slice_fusion.3), channel_id=1, source_target_pairs={{0,8},{4,12},{1,9},{5,13},{2,10},{6,14},{3,11},{7,15},{16,24},{20,... | collective-permute-start | bytes 589832 | tf_op jit(solution)/shard_map/ppermute | solution.py:32
  30.7 1.9 collective-permute-start.7
  32.5 6.4 %multiply_add_fusion.cov_ref = f32[4,5,640,128]{3,2,1,0:T(8,128)} fusion(f32[4,640]{1,0:T(4,128)S(1)} %get-tuple-element.14, f32[5,640,128]{2,1,0:T(8,128)S(1)} %fusion, f32[4,5,128]{2,1,0:T(8,128)S(1)} %sub.101, f32[4,640]{1,0:T(4,128)S(1)} %get-tuple-element.23, f32[4,5,128]{2,1,0:T(8,128)S(1)} %sub.96, f32[4,640]{1,0:T(4,128)S(1)} %get-tuple-element.24, ...), kind=kLoop, calls=%fused_computation.2 | loop fusion | flops 21299200 | bytes 8253520 | tf_op jit(solution)/shard_map/add | solution.py:158
  39.0 0.6 gather_fusion.1
  39.6 0.4 copy.14
  40.0 1.5 broadcast_multiply_fusion.1.val_ref
  41.4 148.4 %shard_map.50 = (f32[4,128,32]{2,1,0:T(8,128)}, f32[4,640,32]{2,1,0:T(8,128)}) custom-call(f32[4,5,640,128]{3,2,1,0:T(8,128)} %multiply_add_fusion.cov_ref, f32[4,640,32]{2,1,0:T(8,128)} %broadcast_multiply_fusion.1.val_ref), custom_call_target="tpu_custom_call" | custom-call | tf_op jit(solution)/shard_map/pallas_call | solution.py:131
  189.9 1.8 broadcast_multiply_fusion
  191.6 0.4 copy.15
  192.1 0.2 copy.20
  192.3 1.3 fusion.2
  193.6 0.1 fusion.17
  193.7 0.1 copy.22
  193.8 1.3 collective-permute-start.8
  195.1 0.1 copy.23
  195.1 1.3 collective-permute-start.9
  196.4 0.1 copy.21
  196.5 5.8 %collective-permute-done.8 = f32[4,3,32,128]{3,2,1,0:T(8,128)S(1)} collective-permute-done((f32[4,3,32,128]{3,2,1,0:T(8,128)S(1)}, f32[4,3,32,128]{3,2,1,0:T(8,128)S(1)}, u32[]{:S(2)}, u32[]{:S(2)}) %collective-permute-start.8) | collective-permute-done | bytes 196640 | tf_op jit(solution)/shard_map/ppermute | solution.py:32
  202.4 9.2 %collective-permute-done.9 = f32[4,3,32,128]{3,2,1,0:T(8,128)S(1)} collective-permute-done((f32[4,3,32,128]{3,2,1,0:T(8,128)S(1)}, f32[4,3,32,128]{3,2,1,0:T(8,128)S(1)}, u32[]{:S(2)}, u32[]{:S(2)}) %collective-permute-start.9) | collective-permute-done | bytes 196640 | tf_op jit(solution)/shard_map/ppermute | solution.py:32
  211.6 1.3 collective-permute-start.10
  212.9 4.5 %collective-permute-start.11 = (f32[4,1,32,128]{3,2,1,0:T(8,128)S(1)}, f32[4,1,32,128]{3,2,1,0:T(8,128)S(1)}, u32[]{:S(2)}, u32[]{:S(2)}) collective-permute-start(f32[4,1,32,128]{3,2,1,0:T(8,128)S(1)} %get-tuple-element.20), channel_id=1, source_target_pairs={{0,2},{1,3},{4,6},{5,7},{8,10},{9,11},{12,14},{13,15},{16,18},{17,... | collective-permute-start | bytes 196616 | tf_op jit(solution)/shard_map/ppermute | solution.py:32
  217.5 0.7 copy.16
  218.2 1.1 collective-permute-done.11
  219.3 0.6 fusion.1
  (31 shorter events, 0.3 us)
Async XLA Ops:
  0.6 14.7 %collective-permute-start = (f32[4,1,2,128]{3,2,1,0:T(2,128)}, f32[4,1,2,128]{3,2,1,0:T(2,128)S(1)}, u32[]{:S(2)}, u32[]{:S(2)}) collective-permute-start(f32[4,1,2,128]{3,2,1,0:T(2,128)} %param.3), channel_id=1, source_target_pairs={{0,2},{1,3},{4,6},{5,7},{8,10},{9,11},{12,14},{13,15},{16,18},{17,... | collective-permute-start | bytes 12296 | tf_op jit(solution)/shard_map/ppermute | solution.py:20
  5.5 10.5 %collective-permute-start.1 = (f32[4,1,2,128]{3,2,1,0:T(2,128)}, f32[4,1,2,128]{3,2,1,0:T(2,128)S(1)}, u32[]{:S(2)}, u32[]{:S(2)}) collective-permute-start(f32[4,1,2,128]{3,2,1,0:T(2,128)} %param.3), channel_id=1, source_target_pairs={{2,0},{3,1},{6,4},{7,5},{10,8},{11,9},{14,12},{15,13},{18,16},{19,... | collective-permute-start | bytes 12296 | tf_op jit(solution)/shard_map/ppermute | solution.py:22
  6.8 19.3 %collective-permute-start.4 = (f32[4,1,32,128]{3,2,1,0:T(8,128)}, f32[4,1,32,128]{3,2,1,0:T(8,128)S(1)}, u32[]{:S(2)}, u32[]{:S(2)}) collective-permute-start(f32[4,1,32,128]{3,2,1,0:T(8,128)} %param.4), channel_id=1, source_target_pairs={{0,2},{1,3},{4,6},{5,7},{8,10},{9,11},{12,14},{13,15},{16,18},{17,... | collective-permute-start | bytes 196616 | tf_op jit(solution)/shard_map/ppermute | solution.py:20
  11.3 15.6 %collective-permute-start.5 = (f32[4,1,32,128]{3,2,1,0:T(8,128)}, f32[4,1,32,128]{3,2,1,0:T(8,128)S(1)}, u32[]{:S(2)}, u32[]{:S(2)}) collective-permute-start(f32[4,1,32,128]{3,2,1,0:T(8,128)} %param.4), channel_id=1, source_target_pairs={{2,0},{3,1},{6,4},{7,5},{10,8},{11,9},{14,12},{15,13},{18,16},{19,... | collective-permute-start | bytes 196616 | tf_op jit(solution)/shard_map/ppermute | solution.py:22
  15.1 24.8 %copy-start.1 = (f32[4,640]{1,0:T(4,128)}, f32[4,640]{1,0:T(4,128)S(1)}, u32[]{:S(2)}) copy-start(f32[4,640]{1,0:T(4,128)S(1)} %get-tuple-element.15) | copy-start | bytes 30724
  16.0 9.3 %collective-permute-start.2 = (f32[4,3,2,128]{3,2,1,0:T(2,128)S(1)}, f32[4,3,2,128]{3,2,1,0:T(2,128)S(1)}, u32[]{:S(2)}, u32[]{:S(2)}) collective-permute-start(f32[4,3,2,128]{3,2,1,0:T(2,128)S(1)} %constant_dynamic-update-slice_fusion), channel_id=1, source_target_pairs={{0,8},{4,12},{1,9},{5,13},{2,10},{6,14},{3,11},{7,15},{16,24},{20,... | collective-permute-start | bytes 36872 | tf_op jit(solution)/shard_map/ppermute | solution.py:32
  20.5 4.9 %collective-permute-start.3 = (f32[4,3,2,128]{3,2,1,0:T(2,128)S(1)}, f32[4,3,2,128]{3,2,1,0:T(2,128)S(1)}, u32[]{:S(2)}, u32[]{:S(2)}) collective-permute-start(f32[4,3,2,128]{3,2,1,0:T(2,128)S(1)} %constant_dynamic-update-slice_fusion), channel_id=1, source_target_pairs={{0,4},{4,8},{8,12},{1,5},{5,9},{9,13},{2,6},{6,10},{10,14},{3,7},{... | collective-permute-start | bytes 36872 | tf_op jit(solution)/shard_map/ppermute | solution.py:32
  27.0 11.9 %collective-permute-start.6 = (f32[4,3,32,128]{3,2,1,0:T(8,128)S(1)}, f32[4,3,32,128]{3,2,1,0:T(8,128)S(1)}, u32[]{:S(2)}, u32[]{:S(2)}) collective-permute-start(f32[4,3,32,128]{3,2,1,0:T(8,128)S(1)} %constant_dynamic-update-slice_fusion.3), channel_id=1, source_target_pairs={{0,8},{4,12},{1,9},{5,13},{2,10},{6,14},{3,11},{7,15},{16,24},{20,... | collective-permute-start | bytes 589832 | tf_op jit(solution)/shard_map/ppermute | solution.py:32
  30.7 8.3 %collective-permute-start.7 = (f32[4,3,32,128]{3,2,1,0:T(8,128)S(1)}, f32[4,3,32,128]{3,2,1,0:T(8,128)S(1)}, u32[]{:S(2)}, u32[]{:S(2)}) collective-permute-start(f32[4,3,32,128]{3,2,1,0:T(8,128)S(1)} %constant_dynamic-update-slice_fusion.3), channel_id=1, source_target_pairs={{0,4},{4,8},{8,12},{1,5},{5,9},{9,13},{2,6},{6,10},{10,14},{3,7},{... | collective-permute-start | bytes 589832 | tf_op jit(solution)/shard_map/ppermute | solution.py:32
  189.9 27.6 %copy-start = (f32[4,128,32]{2,1,0:T(8,128)S(1)}, f32[4,128,32]{2,1,0:T(8,128)}, u32[]{:S(2)}) copy-start(f32[4,128,32]{2,1,0:T(8,128)} %get-tuple-element.4) | copy-start | bytes 196612
  193.8 8.6 %collective-permute-start.8 = (f32[4,3,32,128]{3,2,1,0:T(8,128)S(1)}, f32[4,3,32,128]{3,2,1,0:T(8,128)S(1)}, u32[]{:S(2)}, u32[]{:S(2)}) collective-permute-start(f32[4,3,32,128]{3,2,1,0:T(8,128)S(1)} %bitcast.64), channel_id=1, source_target_pairs={{4,0},{8,4},{12,8},{5,1},{9,5},{13,9},{6,2},{10,6},{14,10},{7,3},{... | collective-permute-start | bytes 589832 | tf_op jit(solution)/shard_map/ppermute | solution.py:32
  195.1 16.4 %collective-permute-start.9 = (f32[4,3,32,128]{3,2,1,0:T(8,128)S(1)}, f32[4,3,32,128]{3,2,1,0:T(8,128)S(1)}, u32[]{:S(2)}, u32[]{:S(2)}) collective-permute-start(f32[4,3,32,128]{3,2,1,0:T(8,128)S(1)} %bitcast.65), channel_id=1, source_target_pairs={{8,0},{12,4},{9,1},{13,5},{10,2},{14,6},{11,3},{15,7},{24,16},{28,... | collective-permute-start | bytes 589832 | tf_op jit(solution)/shard_map/ppermute | solution.py:32
  211.6 6.6 %collective-permute-start.10 = (f32[4,1,32,128]{3,2,1,0:T(8,128)S(1)}, f32[4,1,32,128]{3,2,1,0:T(8,128)S(1)}, u32[]{:S(2)}, u32[]{:S(2)}) collective-permute-start(f32[4,1,32,128]{3,2,1,0:T(8,128)S(1)} %get-tuple-element.19), channel_id=1, source_target_pairs={{2,0},{3,1},{6,4},{7,5},{10,8},{11,9},{14,12},{15,13},{18,16},{19,... | collective-permute-start | bytes 196616 | tf_op jit(solution)/shard_map/ppermute | solution.py:32
  212.9 6.4 %collective-permute-start.11 = (f32[4,1,32,128]{3,2,1,0:T(8,128)S(1)}, f32[4,1,32,128]{3,2,1,0:T(8,128)S(1)}, u32[]{:S(2)}, u32[]{:S(2)}) collective-permute-start(f32[4,1,32,128]{3,2,1,0:T(8,128)S(1)} %get-tuple-element.20), channel_id=1, source_target_pairs={{0,2},{1,3},{4,6},{5,7},{8,10},{9,11},{12,14},{13,15},{16,18},{17,... | collective-permute-start | bytes 196616 | tf_op jit(solution)/shard_map/ppermute | solution.py:32
